TPU v7x, 128 devices: a whole 4x4x4 slice. The times are simulated.
128 devices in a mesh: depth: 4 (over z_lo, core), lat: 32 (over y, z_hi, x).
Axes of the slice: x: 4, y: 4, z: 4 (z_hi: 2, z_lo: 2; z = z_hi * 2 + z_lo), core: 2. Of those that a mesh axis runs over, the one named last changes fastest.
Arguments:
- temp_old: float32 [32, 32, 256, 128], P('depth', 'lat'), may hold values from 0 to 2.5
- material: int32 [32, 32, 256, 128], P('depth', 'lat'), may hold values from 0 to 7
- conduct_table: float32 [8], replicated, may hold values from 0.3 to 3
- capacity_table: float32 [8], replicated, may hold values from 0.5 to 2
- dyn_power: float32 [4, 32, 256, 128], P('depth', 'lat'), may hold values from 0.2 to 4
- leak_ref: float32 [4, 32, 256, 128], P('depth', 'lat'), may hold values from 0.05 to 1
- die_layer: int32 [4], replicated, may hold values from 0 to 31, as said below
Outputs:
- temp_new: float32 [32, 32, 256, 128], P('depth', 'lat')
- die_power: float32 [4, 32, 256, 128], P('depth', 'lat')
Inputs may be any that keep to these rules, and one draw needn't show every extreme that they name: `die_layer`: the 4 entries name different layers of the grid; one die lies on layer 0 and one on the top layer.
All inputs are finite; a program needn't handle non-finite values.
Results may differ from a plain program's by a relative error of at most 0.000059.
Values sent between devices are 32-bit elements; how exact they have to be, the bound alone decides.
No kernel may reach another device: no remote copies, remote signals or barrier semaphores. Data moves between devices by JAX's collectives and lax.ppermute only.
A program may use at most 128 MiB of HBM per device.

v0:
```python
import functools

import jax
import jax.numpy as jnp
from jax import lax
from jax.experimental import pallas as pl
from jax.experimental.pallas import tpu as pltpu
from jax.sharding import PartitionSpec as P

SWEEPS = 6
HALO = SWEEPS
PAD_Y = 8

COND_SLOPE = 0.15
LEAK_SLOPE = 0.5
SINK_CONDUCT = 2.0

INTERPRET = False


def from_behind(block, axis, distance):
    devices = range(lax.axis_size(axis))
    route = [(i - distance, i) for i in devices if i - distance in devices]
    return lax.ppermute(block, axis, route)


def harm(a, b):
    summed = a + b
    return 2.0 * a * b / jnp.where(summed > 0, summed, 1.0)


def lookup(table_ref, material):
    looked = jnp.zeros(material.shape, jnp.float32)
    for entry in range(table_ref.shape[0]):
        looked = jnp.where(material == float(entry), table_ref[entry], looked)
    return looked


def sweep_kernel(nz, ny_total, local_depth, strip,
                 sc_ref, ctab_ref, htab_ref, xb_ref, xc_ref, xa_ref, dl_ref,
                 out_ref, t_s, cond_s, rhs_s, inv_s, gz_s, gx_s, gxl_s, gy_s, gyu_s):
    ze = t_s.shape[1]
    ye = t_s.shape[2]
    xe = t_s.shape[3]
    g = sc_ref[0]
    s = sc_ref[1]
    z0 = g * local_depth - HALO
    row = lax.broadcasted_iota(jnp.int32, (ye, xe), 0)
    lane = lax.broadcasted_iota(jnp.int32, (ye, xe), 1)
    yg = s * strip + row - PAD_Y
    yvalid = (yg >= 0) & (yg < ny_total) & (row >= PAD_Y - HALO) & (row < PAD_Y + strip + HALO)

    def tables(l, temp, mat):
        zg = z0 + l
        valid = yvalid & (zg >= 0) & (zg < nz)
        cval = lookup(ctab_ref, mat)
        hval = lookup(htab_ref, mat)
        cond = jnp.where(valid, cval * jnp.exp(-COND_SLOPE * temp), 0.0)
        t_s[0, l] = temp
        cond_s[l] = cond
        inv_s[l] = hval
        rhs_s[l] = hval * temp

    def below(i, c):
        tables(i, xb_ref[0, i], xb_ref[1, i])
        return c

    def centre(i, c):
        tables(HALO + i, xc_ref[0, i], xc_ref[1, i])
        return c

    def above(i, c):
        tables(HALO + local_depth + i, xa_ref[0, i], xa_ref[1, i])
        return c

    lax.fori_loop(0, HALO, below, 0)
    lax.fori_loop(0, local_depth, centre, 0)
    lax.fori_loop(0, HALO, above, 0)

    for d in range(dl_ref.shape[0]):
        rel = sc_ref[2 + d] - z0
        relc = jnp.clip(rel, 0, ze - 1)

        @pl.when((rel >= 0) & (rel < ze))
        def _():
            power = dl_ref[d, 0] + dl_ref[d, 1] * jnp.exp(LEAK_SLOPE * t_s[0, relc])
            rhs_s[relc] = inv_s[relc] * t_s[0, relc] + power

    def faces_z(l, c):
        gz_s[l] = harm(cond_s[l], cond_s[l + 1])
        return c

    lax.fori_loop(0, ze - 1, faces_z, 0)
    gz_s[ze - 1] = jnp.zeros((ye, xe), jnp.float32)

    def faces(l, c):
        cc = cond_s[l]
        gx = harm(cc, pltpu.roll(cc, xe - 1, 1))
        gx = jnp.where(lane == xe - 1, 0.0, gx)
        gy = harm(cc, pltpu.roll(cc, ye - 1, 0))
        gy = jnp.where(row == ye - 1, 0.0, gy)
        gxl = pltpu.roll(gx, 1, 1)
        gyu = pltpu.roll(gy, 1, 0)
        gx_s[l] = gx
        gxl_s[l] = gxl
        gy_s[l] = gy
        gyu_s[l] = gyu
        lm = jnp.maximum(l - 1, 0)
        gzm = jnp.where(l > 0, gz_s[lm], 0.0)
        sink = jnp.where(z0 + l == 0, SINK_CONDUCT, 0.0)
        diag = inv_s[l] + (gz_s[l] + gzm + gx + gxl + gy + gyu) + sink
        inv_s[l] = 1.0 / diag
        return c

    lax.fori_loop(0, ze, faces, 0)

    def relax(src, l):
        t = t_s[src, l]
        coupled = (gz_s[l] * t_s[src, l + 1] + gz_s[l - 1] * t_s[src, l - 1]
                   + gx_s[l] * pltpu.roll(t, xe - 1, 1) + gxl_s[l] * pltpu.roll(t, 1, 1)
                   + gy_s[l] * pltpu.roll(t, ye - 1, 0) + gyu_s[l] * pltpu.roll(t, 1, 0))
        return (rhs_s[l] + coupled) * inv_s[l]

    for k in range(1, SWEEPS):
        src, dst = (k - 1) % 2, k % 2

        def body(l, c, src=src, dst=dst):
            t_s[dst, l] = relax(src, l)
            return c

        lax.fori_loop(k, ze - k, body, 0)

    last = (SWEEPS - 1) % 2

    def final(i, c):
        new = relax(last, HALO + i)
        out_ref[i] = new[PAD_Y:PAD_Y + strip]
        return c

    lax.fori_loop(0, local_depth, final, 0)


def local(temp_old, material, conduct_table, capacity_table, dyn_power, leak_ref, die_layer):
    temp_start = temp_old[:, 0]
    cells_mat = material[:, 0]
    local_depth, nx, strip = temp_start.shape
    depth_n = lax.axis_size("depth")
    lat_n = lax.axis_size("lat")
    nz = local_depth * depth_n
    g = lax.axis_index("depth")
    s = lax.axis_index("lat")
    first_layer = g * local_depth
    layer_ids = first_layer + lax.iota(jnp.int32, local_depth)

    select = (die_layer[:, None] == layer_ids[None, :]).astype(jnp.float32)
    picked = jnp.einsum("dz,zxy->dxy", select, temp_start, precision=lax.Precision.HIGHEST)
    die_temp = lax.psum_scatter(picked, "depth", scatter_dimension=0, tiled=True)
    die_power = dyn_power[:, 0] + leak_ref[:, 0] * jnp.exp(LEAK_SLOPE * die_temp)

    tt = jnp.transpose(temp_start, (0, 2, 1))
    mt = jnp.transpose(cells_mat, (0, 2, 1)).astype(jnp.float32)
    dt = jnp.transpose(dyn_power[:, 0], (0, 2, 1))
    lt = jnp.transpose(leak_ref[:, 0], (0, 2, 1))
    fields = jnp.concatenate([tt, mt, dt, lt], axis=0)
    lo = from_behind(fields[:, strip - HALO:], "lat", 1)
    hi = from_behind(fields[:, :HALO], "lat", -1)
    nf = fields.shape[0]
    ye = PAD_Y + strip + HALO + (-(PAD_Y + strip + HALO)) % 8
    zpad_lo = jnp.zeros((nf, PAD_Y - HALO, nx), jnp.float32)
    zpad_hi = jnp.zeros((nf, ye - (PAD_Y + strip + HALO), nx), jnp.float32)
    wide = jnp.concatenate([zpad_lo, lo, fields, hi, zpad_hi], axis=1)
    tm = wide[:2 * local_depth].reshape(2, local_depth, ye, nx)
    dl = wide[2 * local_depth:].reshape(2, ye, nx)

    xb = from_behind(tm[:, local_depth - HALO:], "depth", 1)
    xa = from_behind(tm[:, :HALO], "depth", -1)
    dl_all = lax.all_gather(dl, "depth", axis=0, tiled=False)

    sc = jnp.concatenate([jnp.stack([g, s]).astype(jnp.int32), die_layer.astype(jnp.int32)])
    ze = local_depth + 2 * HALO
    smem = pl.BlockSpec(memory_space=pltpu.MemorySpace.SMEM)
    vmem = pl.BlockSpec(memory_space=pltpu.MemorySpace.VMEM)
    full = (ze, ye, nx)
    kern = functools.partial(sweep_kernel, nz, strip * lat_n, local_depth, strip)
    out = pl.pallas_call(
        kern,
        out_shape=jax.ShapeDtypeStruct((local_depth, strip, nx), jnp.float32),
        in_specs=[smem, smem, smem, vmem, vmem, vmem, vmem],
        out_specs=vmem,
        scratch_shapes=[pltpu.VMEM((2,) + full, jnp.float32)] + [pltpu.VMEM(full, jnp.float32)] * 8,
        compiler_params=pltpu.CompilerParams(vmem_limit_bytes=60 * 1024 * 1024),
        interpret=INTERPRET,
    )(sc, conduct_table, capacity_table, xb, tm, xa, dl_all)
    temp_new = jnp.transpose(out, (0, 2, 1))
    return (temp_new[:, None], die_power[:, None])


def solution(mesh):
    return jax.shard_map(
        local,
        mesh=mesh,
        in_specs=(
            P("depth", "lat", None, None),
            P("depth", "lat", None, None),
            P(),
            P(),
            P("depth", "lat", None, None),
            P("depth", "lat", None, None),
            P(),
        ),
        out_specs=(P("depth", "lat", None, None), P("depth", "lat", None, None)),
        check_vma=False,
    )
```

profile of v0, /device:TPU:56, one launch (start us, length us, event | category | flops | bytes accessed | tf_op | source)
XLA Modules:
  0.0 114.8 jit_solution(4290308888477413516)
XLA Ops:
  7.3 2.5 %fusion = f32[4,256,128]{2,0,1:T(4,128)S(1)} fusion(f32[8,256,128]{2,1,0:T(8,128)} %bitcast.35, s32[8]{0:T(128)S(1)} %iota_add_fusion, s32[4]{0:T(128)} %param.13), kind=kOutput, calls=%fused_computation.1 | convolution fusion | flops 12582944 | bytes 1572912 | tf_op jit(solution)/shard_map/dz,zxy->dxy/dot_general | solution.py:156
  9.8 0.8 copy.20
  11.2 0.8 copy.18
  12.3 1.1 pad_maximum_fusion
  13.5 7.3 %collective-permute-start.1 = (f32[18,6,256]{2,1,0:T(8,128)S(1)}, f32[18,6,256]{2,1,0:T(8,128)S(1)}, u32[]{:S(2)}, u32[]{:S(2)}) collective-permute-start(f32[18,6,256]{2,1,0:T(8,128)S(1)} %get-tuple-element.8), channel_id=1, source_target_pairs={{1,0},{2,1},{3,2},{4,3},{5,4},{6,5},{7,6},{8,7},{9,8},{10,9},{11,1... | collective-permute-start | bytes 331784 | tf_op jit(solution)/shard_map/ppermute | solution.py:24
  20.8 1.9 %collective-permute-start = (f32[18,6,256]{2,1,0:T(8,128)S(1)}, f32[18,6,256]{2,1,0:T(8,128)S(1)}, u32[]{:S(2)}, u32[]{:S(2)}) collective-permute-start(f32[18,6,256]{2,1,0:T(8,128)S(1)} %get-tuple-element.9), channel_id=1, source_target_pairs={{0,1},{1,2},{2,3},{3,4},{4,5},{5,6},{6,7},{7,8},{8,9},{9,10},{10,1... | collective-permute-start | bytes 331784 | tf_op jit(solution)/shard_map/ppermute | solution.py:24
  22.7 1.2 %collective-permute-done.1 = f32[18,6,256]{2,1,0:T(8,128)S(1)} collective-permute-done((f32[18,6,256]{2,1,0:T(8,128)S(1)}, f32[18,6,256]{2,1,0:T(8,128)S(1)}, u32[]{:S(2)}, u32[]{:S(2)}) %collective-permute-start.1) | collective-permute-done | bytes 110624 | tf_op jit(solution)/shard_map/ppermute | solution.py:24
  23.9 8.7 %collective-permute-done = f32[18,6,256]{2,1,0:T(8,128)S(1)} collective-permute-done((f32[18,6,256]{2,1,0:T(8,128)S(1)}, f32[18,6,256]{2,1,0:T(8,128)S(1)}, u32[]{:S(2)}, u32[]{:S(2)}) %collective-permute-start) | collective-permute-done | bytes 110624 | tf_op jit(solution)/shard_map/ppermute | solution.py:24
  32.6 5.2 %concatenate.11 = f32[18,144,256]{2,1,0:T(8,128)} concatenate(f32[18,2,256]{2,1,0:T(2,128)S(1)} %broadcast.8, f32[18,6,256]{2,1,0:T(8,128)S(1)} %collective-permute-done, f32[18,128,256]{2,1,0:T(8,128)S(1)} %pad_maximum_fusion, f32[18,6,256]{2,1,0:T(8,128)S(1)} %collective-permute-done.1, f32[18,2,256]{2,1,0:T(2,128)S(1)} %broadcast.8), dimensions={1} | concatenate | bytes 5308416 | tf_op jit(solution)/shard_map/concatenate | solution.py:171
  37.8 1.7 %slice.29 = f32[2,144,256]{2,1,0:T(8,128)} slice(f32[18,144,256]{2,1,0:T(8,128)} %concatenate.11), slice={[16:18], [0:144], [0:256]} | slice | bytes 589824 | tf_op jit(solution)/shard_map/slice | solution.py:173
  39.5 1.8 %slice.26 = f32[16,144,256]{2,1,0:T(8,128)S(1)} slice(f32[18,144,256]{2,1,0:T(8,128)} %concatenate.11), slice={[0:16], [0:144], [0:256]} | slice | bytes 4718592 | tf_op jit(solution)/shard_map/slice | solution.py:172
  41.3 0.4 fusion.8
  41.7 1.0 copy-done
  42.7 1.9 %collective-permute-start.3 = (f32[2,6,144,256]{3,2,1,0:T(8,128)S(1)}, f32[2,6,144,256]{3,2,1,0:T(8,128)}, u32[]{:S(2)}, u32[]{:S(2)}) collective-permute-start(f32[2,6,144,256]{3,2,1,0:T(8,128)S(1)} %get-tuple-element.6), channel_id=1, source_target_pairs={{32,0},{64,32},{96,64},{33,1},{65,33},{97,65},{34,2},{66,34},{98,6... | collective-permute-start | bytes 5308424 | tf_op jit(solution)/shard_map/ppermute | solution.py:24
  44.7 3.6 %collective-permute-start.2 = (f32[2,6,144,256]{3,2,1,0:T(8,128)S(1)}, f32[2,6,144,256]{3,2,1,0:T(8,128)}, u32[]{:S(2)}, u32[]{:S(2)}) collective-permute-start(f32[2,6,144,256]{3,2,1,0:T(8,128)S(1)} %get-tuple-element.7), channel_id=1, source_target_pairs={{0,32},{32,64},{64,96},{1,33},{33,65},{65,97},{2,34},{34,66},{66,9... | collective-permute-start | bytes 5308424 | tf_op jit(solution)/shard_map/ppermute | solution.py:24
  48.3 0.6 pad_add_fusion.sc_ref
  48.9 1.7 %copy.21 = f32[1,256,128]{1,2,0:T(8,128)} copy(f32[1,256,128]{2,1,0:T(8,128)} %reduce-scatter.2.cloned.1.call-done) | data formatting | bytes 262144 | tf_op jit(solution)/shard_map/reduce_scatter | solution.py:157
  50.6 1.7 %fusion.3 = f32[1,1,256,128]{2,3,1,0:T(8,128)} fusion(f32[1,1,256,128]{2,3,1,0:T(8,128)} %copy.18, f32[1,1,256,128]{2,3,1,0:T(8,128)} %copy-done.2, f32[1,256,128]{1,2,0:T(8,128)} %copy.21), kind=kLoop, calls=%fused_computation.6 | loop fusion | flops 98304 | bytes 524288 | tf_op jit(solution)/shard_map/broadcast_in_dim | solution.py:195
  52.3 1.7 %copy.23 = f32[1,1,256,128]{3,2,1,0:T(8,128)} copy(f32[1,1,256,128]{2,3,1,0:T(8,128)} %fusion.3) | data formatting | bytes 262144
  54.0 14.6 %all-gather.3.cloned.1.call-done = f32[8,144,256]{2,1,0:T(8,128)} async-done(((f32[2,144,256]{2,1,0:T(8,128)}), f32[8,144,256]{2,1,0:T(8,128)}) %all-gather.3.cloned.1.call-update) | async-done | bytes 1179664 | tf_op jit(solution)/shard_map/all_gather | solution.py:177
  68.6 5.6 %collective-permute-done.3.xa_ref = f32[2,6,144,256]{3,2,1,0:T(8,128)} collective-permute-done((f32[2,6,144,256]{3,2,1,0:T(8,128)S(1)}, f32[2,6,144,256]{3,2,1,0:T(8,128)}, u32[]{:S(2)}, u32[]{:S(2)}) %collective-permute-start.3) | collective-permute-done | bytes 1769504 | tf_op jit(solution)/shard_map/ppermute | solution.py:24
  74.1 4.0 %collective-permute-done.2.xb_ref = f32[2,6,144,256]{3,2,1,0:T(8,128)} collective-permute-done((f32[2,6,144,256]{3,2,1,0:T(8,128)S(1)}, f32[2,6,144,256]{3,2,1,0:T(8,128)}, u32[]{:S(2)}, u32[]{:S(2)}) %collective-permute-start.2) | collective-permute-done | bytes 1769504 | tf_op jit(solution)/shard_map/ppermute | solution.py:24
  78.1 27.4 %shard_map.86 = f32[8,128,256]{2,1,0:T(8,128)} custom-call(s32[6]{0:T(128)} %pad_add_fusion.sc_ref, f32[8]{0:T(128)} %ctab_ref.1, f32[8]{0:T(128)} %htab_ref.1, f32[2,6,144,256]{3,2,1,0:T(8,128)} %collective-permute-done.2.xb_ref, f32[2,8,144,256]{3,2,1,0:T(8,128)} %bitcast.33, f32[2,6,144,256]{3,2,1,0:T(8,128)} %collective-permute-done.3.xa_ref, ...), custom_call_target="tpu_custom_call" | custom-call | tf_op jit(solution)/shard_map/pallas_call | solution.py:185
  105.5 2.5 %copy.22 = f32[8,1,256,128]{3,2,1,0:T(8,128)} copy(f32[8,1,256,128]{2,3,0,1:T(8,128)} %bitcast.34) | data formatting | bytes 2097152
  (25 shorter events, 1.0 us)
Async XLA Ops:
  7.2 3.5 %copy-start.1 = (f32[8,1,256,128]{3,2,1,0:T(8,128)S(1)}, f32[8,1,256,128]{3,2,1,0:T(8,128)}, u32[]{:S(2)}) copy-start(f32[8,1,256,128]{3,2,1,0:T(8,128)} %param.7) | copy-start | bytes 3145732
  7.2 41.8 %reduce-scatter.2.cloned.1.call-start = ((), (), s32[]{:S(2)}) async-start(), calls=%async_computation.1 | async-start | bytes 655360 | tf_op jit(solution)/shard_map/reduce_scatter | solution.py:157
  7.2 3.8 %copy-start.4 = (f32[1,1,256,128]{3,2,1,0:T(8,128)S(1)}, f32[1,1,256,128]{3,2,1,0:T(8,128)}, u32[]{:S(2)}) copy-start(f32[1,1,256,128]{3,2,1,0:T(8,128)} %param.11) | copy-start | bytes 393220
  9.7 1.4 %copy-start.5 = (f32[1,1,256,128]{3,2,1,0:T(8,128)S(1)}, f32[1,1,256,128]{3,2,1,0:T(8,128)}, u32[]{:S(2)}) copy-start(f32[1,1,256,128]{3,2,1,0:T(8,128)} %param.12) | copy-start | bytes 393220
  9.8 2.2 %copy-start.3 = (s32[8,1,256,128]{3,2,1,0:T(8,128)S(1)}, s32[8,1,256,128]{3,2,1,0:T(8,128)}, u32[]{:S(2)}) copy-start(s32[8,1,256,128]{3,2,1,0:T(8,128)} %param.8) | copy-start | bytes 3145732
  10.6 57.9 %all-gather.3.cloned.1.call-start = ((), (), s32[]{:S(2)}) async-start(), calls=%async_computation.2 | async-start | bytes 1474560 | tf_op jit(solution)/shard_map/all_gather | solution.py:177
  11.1 2.3 %copy-start.2 = (f32[1,1,256,128]{2,3,1,0:T(8,128)}, f32[1,1,256,128]{2,3,1,0:T(8,128)S(1)}, u32[]{:S(2)}) copy-start(f32[1,1,256,128]{2,3,1,0:T(8,128)S(1)} %copy.17) | copy-start | bytes 393220
  13.5 10.4 %collective-permute-start.1 = (f32[18,6,256]{2,1,0:T(8,128)S(1)}, f32[18,6,256]{2,1,0:T(8,128)S(1)}, u32[]{:S(2)}, u32[]{:S(2)}) collective-permute-start(f32[18,6,256]{2,1,0:T(8,128)S(1)} %get-tuple-element.8), channel_id=1, source_target_pairs={{1,0},{2,1},{3,2},{4,3},{5,4},{6,5},{7,6},{8,7},{9,8},{10,9},{11,1... | collective-permute-start | bytes 331784 | tf_op jit(solution)/shard_map/ppermute | solution.py:24
  20.8 11.8 %collective-permute-start = (f32[18,6,256]{2,1,0:T(8,128)S(1)}, f32[18,6,256]{2,1,0:T(8,128)S(1)}, u32[]{:S(2)}, u32[]{:S(2)}) collective-permute-start(f32[18,6,256]{2,1,0:T(8,128)S(1)} %get-tuple-element.9), channel_id=1, source_target_pairs={{0,1},{1,2},{2,3},{3,4},{4,5},{5,6},{6,7},{7,8},{8,9},{9,10},{10,1... | collective-permute-start | bytes 331784 | tf_op jit(solution)/shard_map/ppermute | solution.py:24
  41.3 1.4 %copy-start = (f32[16,144,256]{2,1,0:T(8,128)}, f32[16,144,256]{2,1,0:T(8,128)S(1)}, u32[]{:S(2)}) copy-start(f32[16,144,256]{2,1,0:T(8,128)S(1)} %slice.26) | copy-start | bytes 7077892
  41.3 7.0 %copy-start.6 = (s32[4]{0:T(128)S(1)}, s32[4]{0:T(128)}, u32[]{:S(2)}) copy-start(s32[4]{0:T(128)} %param.13) | copy-start | bytes 52
  42.7 31.4 %collective-permute-start.3 = (f32[2,6,144,256]{3,2,1,0:T(8,128)S(1)}, f32[2,6,144,256]{3,2,1,0:T(8,128)}, u32[]{:S(2)}, u32[]{:S(2)}) collective-permute-start(f32[2,6,144,256]{3,2,1,0:T(8,128)S(1)} %get-tuple-element.6), channel_id=1, source_target_pairs={{32,0},{64,32},{96,64},{33,1},{65,33},{97,65},{34,2},{66,34},{98,6... | collective-permute-start | bytes 5308424 | tf_op jit(solution)/shard_map/ppermute | solution.py:24
  44.7 33.4 %collective-permute-start.2 = (f32[2,6,144,256]{3,2,1,0:T(8,128)S(1)}, f32[2,6,144,256]{3,2,1,0:T(8,128)}, u32[]{:S(2)}, u32[]{:S(2)}) collective-permute-start(f32[2,6,144,256]{3,2,1,0:T(8,128)S(1)} %get-tuple-element.7), channel_id=1, source_target_pairs={{0,32},{32,64},{64,96},{1,33},{33,65},{65,97},{2,34},{34,66},{66,9... | collective-permute-start | bytes 5308424 | tf_op jit(solution)/shard_map/ppermute | solution.py:24
Sparse Core Ops, SparseCore 0:
  10.9 21.8 reduce-scatter.1
  44.8 23.7 all-gather.2
where the time goes:
time: 115 us
  waiting for transfers between devices  34 us (30%)
  Pallas kernels  27.4 us (24%)
  local copies, waits for them, and re-layouts  18.4 us (16%)
  starting transfers between devices  14.8 us (13%)
  between operations  14.3 us (12%)
  other arithmetic  3.52 us (3%)
  matrix products  2.49 us (2%)
    pallas_call x1, Pallas kernels, local(): pl.pallas_call(kern, out_shape=jax.ShapeDtypeStruct((local_depth, strip,...  27.4 us
    ppermute x4, waiting for transfers between devices, from_behind(): return lax.ppermute(block, axis, route)  19.4 us
    ppermute x4, starting transfers between devices, from_behind(): return lax.ppermute(block, axis, route)  14.7 us
    all_gather x1, waiting for transfers between devices, local(): dl_all = lax.all_gather(dl, 'depth', axis=0, tiled=False)  14.6 us
    unnamed x20, local copies, waits for them, and re-layouts  6.78 us
    concatenate x1, local copies, waits for them, and re-layouts, local(): wide = jnp.concatenate([zpad_lo, lo, fields, hi, zpad_hi], axis=1)  5.17 us
    dot_general x1, matrix products, local(): jnp.einsum('dz,zxy->dxy', select, temp_start, precision=lax.Precision.HIG...  2.49 us
  transfers between devices with their start and end apart: 6, of which 5 were waited for; matrix products, arithmetic and copies ran while one was open for 15% of the time, Pallas kernels for 0%

commit v1 on v0

--- a/solution.py
+++ b/solution.py
@@ -37,8 +37,9 @@
 
 
 def sweep_kernel(nz, ny_total, local_depth, strip,
-                 sc_ref, ctab_ref, htab_ref, xb_ref, xc_ref, xa_ref, dl_ref,
-                 out_ref, t_s, cond_s, rhs_s, inv_s, gz_s, gx_s, gxl_s, gy_s, gyu_s):
+                 sc_ref, ctab_ref, htab_ref, xc_ref, ylo_ref, yhi_ref, xb_ref, xa_ref,
+                 cb_ref, ca_ref, dc_ref, dlo_ref, dhi_ref,
+                 out_ref, t_s, cond_s, rhs_s, inv_s, gz_s, gx_s, gxl_s, gy_s, gyu_s, dl_s):
     ze = t_s.shape[1]
     ye = t_s.shape[2]
     xe = t_s.shape[3]
@@ -49,41 +50,58 @@
     lane = lax.broadcasted_iota(jnp.int32, (ye, xe), 1)
     yg = s * strip + row - PAD_Y
     yvalid = (yg >= 0) & (yg < ny_total) & (row >= PAD_Y - HALO) & (row < PAD_Y + strip + HALO)
-
-    def tables(l, temp, mat):
+    top = PAD_Y + strip + HALO
+    zlo = jnp.zeros((PAD_Y - HALO, xe), jnp.float32)
+    zhi = jnp.zeros((ye - top, xe), jnp.float32)
+
+    def put(dst, centre, lo, hi):
+        dst[PAD_Y - HALO:PAD_Y] = lo
+        dst[PAD_Y:PAD_Y + strip] = centre
+        dst[PAD_Y + strip:top] = hi
+        dst[0:PAD_Y - HALO] = zlo
+        dst[top:ye] = zhi
+
+    def tables(l, parts):
+        for f, dst in ((0, t_s.at[0, l]), (1, cond_s.at[l])):
+            put(dst, *parts[f])
+        temp = t_s[0, l]
+        mat = cond_s[l]
         zg = z0 + l
         valid = yvalid & (zg >= 0) & (zg < nz)
         cval = lookup(ctab_ref, mat)
         hval = lookup(htab_ref, mat)
         cond = jnp.where(valid, cval * jnp.exp(-COND_SLOPE * temp), 0.0)
-        t_s[0, l] = temp
         cond_s[l] = cond
         inv_s[l] = hval
         rhs_s[l] = hval * temp
 
     def below(i, c):
-        tables(i, xb_ref[0, i], xb_ref[1, i])
+        tables(i, [(xb_ref[f, i], cb_ref[f, i, :HALO], cb_ref[f, i, HALO:]) for f in range(2)])
         return c
 
     def centre(i, c):
-        tables(HALO + i, xc_ref[0, i], xc_ref[1, i])
+        tables(HALO + i, [(xc_ref[f, i], ylo_ref[f * local_depth + i], yhi_ref[f * local_depth + i])
+                          for f in range(2)])
         return c
 
     def above(i, c):
-        tables(HALO + local_depth + i, xa_ref[0, i], xa_ref[1, i])
+        tables(HALO + local_depth + i,
+               [(xa_ref[f, i], ca_ref[f, i, :HALO], ca_ref[f, i, HALO:]) for f in range(2)])
         return c
 
     lax.fori_loop(0, HALO, below, 0)
     lax.fori_loop(0, local_depth, centre, 0)
     lax.fori_loop(0, HALO, above, 0)
 
-    for d in range(dl_ref.shape[0]):
+    for d in range(dc_ref.shape[0]):
         rel = sc_ref[2 + d] - z0
         relc = jnp.clip(rel, 0, ze - 1)
 
         @pl.when((rel >= 0) & (rel < ze))
         def _():
-            power = dl_ref[d, 0] + dl_ref[d, 1] * jnp.exp(LEAK_SLOPE * t_s[0, relc])
+            for f in range(2):
+                put(dl_s.at[f], dc_ref[d, f], dlo_ref[2 * d + f], dhi_ref[2 * d + f])
+            power = dl_s[0] + dl_s[1] * jnp.exp(LEAK_SLOPE * t_s[0, relc])
             rhs_s[relc] = inv_s[relc] * t_s[0, relc] + power
 
     def faces_z(l, c):
@@ -159,25 +177,28 @@
 
     tt = jnp.transpose(temp_start, (0, 2, 1))
     mt = jnp.transpose(cells_mat, (0, 2, 1)).astype(jnp.float32)
-    dt = jnp.transpose(dyn_power[:, 0], (0, 2, 1))
-    lt = jnp.transpose(leak_ref[:, 0], (0, 2, 1))
-    fields = jnp.concatenate([tt, mt, dt, lt], axis=0)
-    lo = from_behind(fields[:, strip - HALO:], "lat", 1)
-    hi = from_behind(fields[:, :HALO], "lat", -1)
-    nf = fields.shape[0]
-    ye = PAD_Y + strip + HALO + (-(PAD_Y + strip + HALO)) % 8
-    zpad_lo = jnp.zeros((nf, PAD_Y - HALO, nx), jnp.float32)
-    zpad_hi = jnp.zeros((nf, ye - (PAD_Y + strip + HALO), nx), jnp.float32)
-    wide = jnp.concatenate([zpad_lo, lo, fields, hi, zpad_hi], axis=1)
-    tm = wide[:2 * local_depth].reshape(2, local_depth, ye, nx)
-    dl = wide[2 * local_depth:].reshape(2, ye, nx)
+    tm = jnp.stack([tt, mt])
+    dl = jnp.transpose(jnp.concatenate([dyn_power[:, 0], leak_ref[:, 0]]), (0, 2, 1))
 
     xb = from_behind(tm[:, local_depth - HALO:], "depth", 1)
     xa = from_behind(tm[:, :HALO], "depth", -1)
-    dl_all = lax.all_gather(dl, "depth", axis=0, tiled=False)
+    rows = tm.reshape(2 * local_depth, strip, nx)
+    ylo = from_behind(rows[:, strip - HALO:], "lat", 1)
+    yhi = from_behind(rows[:, :HALO], "lat", -1)
+    dc = lax.all_gather(dl, "depth", axis=0, tiled=False)
+
+    ylo2 = ylo.reshape(2, local_depth, HALO, nx)
+    yhi2 = yhi.reshape(2, local_depth, HALO, nx)
+    side = jnp.concatenate([ylo2, yhi2], axis=2)
+    cb = from_behind(side[:, local_depth - HALO:], "depth", 1)
+    ca = from_behind(side[:, :HALO], "depth", -1)
+    drows = dc.reshape(-1, strip, nx)
+    dlo = from_behind(drows[:, strip - HALO:], "lat", 1)
+    dhi = from_behind(drows[:, :HALO], "lat", -1)
 
     sc = jnp.concatenate([jnp.stack([g, s]).astype(jnp.int32), die_layer.astype(jnp.int32)])
     ze = local_depth + 2 * HALO
+    ye = PAD_Y + strip + HALO + (-(PAD_Y + strip + HALO)) % 8
     smem = pl.BlockSpec(memory_space=pltpu.MemorySpace.SMEM)
     vmem = pl.BlockSpec(memory_space=pltpu.MemorySpace.VMEM)
     full = (ze, ye, nx)
@@ -185,12 +206,13 @@
     out = pl.pallas_call(
         kern,
         out_shape=jax.ShapeDtypeStruct((local_depth, strip, nx), jnp.float32),
-        in_specs=[smem, smem, smem, vmem, vmem, vmem, vmem],
+        in_specs=[smem] * 3 + [vmem] * 10,
         out_specs=vmem,
-        scratch_shapes=[pltpu.VMEM((2,) + full, jnp.float32)] + [pltpu.VMEM(full, jnp.float32)] * 8,
+        scratch_shapes=([pltpu.VMEM((2,) + full, jnp.float32)] + [pltpu.VMEM(full, jnp.float32)] * 8
+                        + [pltpu.VMEM((2, ye, nx), jnp.float32)]),
         compiler_params=pltpu.CompilerParams(vmem_limit_bytes=60 * 1024 * 1024),
         interpret=INTERPRET,
-    )(sc, conduct_table, capacity_table, xb, tm, xa, dl_all)
+    )(sc, conduct_table, capacity_table, tm, ylo, yhi, xb, xa, cb, ca, dc, dlo, dhi)
     temp_new = jnp.transpose(out, (0, 2, 1))
     return (temp_new[:, None], die_power[:, None])
 

time: 115 us -> 112 us (0.974)
  the two profiles are of different devices: /device:TPU:56 before, /device:TPU:14 now
where the time goes in v1:
time: 112 us; the launch traced here: 111 us
  waiting for transfers between devices  32.7 us (29%)
  Pallas kernels  27.6 us (25%)
  starting transfers between devices  22.6 us (20%)
  between operations  14.3 us (13%)
  local copies, waits for them, and re-layouts  7.7 us (7%)
  other arithmetic  3.79 us (3%)
  matrix products  2.45 us (2%)
    pallas_call x1, Pallas kernels, local(): pl.pallas_call(kern, out_shape=jax.ShapeDtypeStruct((local_depth, strip,...  27.6 us
    ppermute x8, starting transfers between devices, from_behind(): return lax.ppermute(block, axis, route)  22.5 us
    ppermute x8, waiting for transfers between devices, from_behind(): return lax.ppermute(block, axis, route)  16.4 us
    all_gather x1, waiting for transfers between devices, local(): dc = lax.all_gather(dl, 'depth', axis=0, tiled=False)  16.3 us
    unnamed x26, local copies, waits for them, and re-layouts  4.97 us
    dot_general x1, matrix products, local(): jnp.einsum('dz,zxy->dxy', select, temp_start, precision=lax.Precision.HIG...  2.45 us
    another operation x3, other arithmetic, local(): tm = jnp.stack([tt, mt])  2.32 us
  transfers between devices with their start and end apart: 10, of which 4 were waited for; matrix products, arithmetic and copies ran while one was open for 7% of the time, Pallas kernels for 0%

profile of v1, /device:TPU:14, one launch (start us, length us, event | category | flops | bytes accessed | tf_op | source)
XLA Modules:
  0.0 111.2 jit_solution(5942099337506465243)
XLA Ops:
  7.3 2.4 %fusion.2 = f32[4,256,128]{2,0,1:T(4,128)S(1)} fusion(f32[8,256,128]{2,1,0:T(8,128)} %bitcast.36, s32[8]{0:T(128)S(1)} %iota_add_fusion, s32[4]{0:T(128)} %param.13), kind=kOutput, calls=%fused_computation.7 | convolution fusion | flops 12582944 | bytes 1572912 | tf_op jit(solution)/shard_map/dz,zxy->dxy/dot_general | solution.py:174
  9.7 0.8 copy.27
  10.9 0.7 maximum_bitcast_fusion
  11.6 0.3 copy.22
  12.6 2.1 %fusion.1 = (f32[2,6,128,256]{3,2,1,0:T(8,128)}, f32[2,6,128,256]{3,2,1,0:T(8,128)}) fusion(f32[1,8,128,256]{3,2,1,0:T(8,128)S(1)} %bitcast.33, f32[1,8,128,256]{3,2,1,0:T(8,128)S(1)} %convert_bitcast_fusion), kind=kLoop, calls=%fused_computation.6 | loop fusion | flops 786432 | bytes 5242880 | tf_op jit(solution)/shard_map/stack | solution.py:180
  14.6 2.9 %collective-permute-start.2 = (f32[2,6,128,256]{3,2,1,0:T(8,128)}, f32[2,6,128,256]{3,2,1,0:T(8,128)}, u32[]{:S(2)}, u32[]{:S(2)}) collective-permute-start(f32[2,6,128,256]{3,2,1,0:T(8,128)} %get-tuple-element.9), channel_id=1, source_target_pairs={{0,32},{32,64},{64,96},{1,33},{33,65},{65,97},{2,34},{34,66},{66,9... | collective-permute-start | bytes 4718600 | tf_op jit(solution)/shard_map/ppermute | solution.py:24
  17.5 1.4 %collective-permute-start.3 = (f32[2,6,128,256]{3,2,1,0:T(8,128)}, f32[2,6,128,256]{3,2,1,0:T(8,128)}, u32[]{:S(2)}, u32[]{:S(2)}) collective-permute-start(f32[2,6,128,256]{3,2,1,0:T(8,128)} %get-tuple-element.8), channel_id=1, source_target_pairs={{32,0},{64,32},{96,64},{33,1},{65,33},{97,65},{34,2},{66,34},{98,6... | collective-permute-start | bytes 4718600 | tf_op jit(solution)/shard_map/ppermute | solution.py:24
  19.2 5.7 %collective-permute-start = (f32[16,6,256]{2,1,0:T(8,128)S(1)}, f32[16,6,256]{2,1,0:T(8,128)S(1)}, u32[]{:S(2)}, u32[]{:S(2)}) collective-permute-start(f32[16,6,256]{2,1,0:T(8,128)S(1)} %get-tuple-element.11), channel_id=1, source_target_pairs={{0,1},{1,2},{2,3},{3,4},{4,5},{5,6},{6,7},{7,8},{8,9},{9,10},{10,1... | collective-permute-start | bytes 294920 | tf_op jit(solution)/shard_map/ppermute | solution.py:24
  24.9 1.9 %collective-permute-start.1 = (f32[16,6,256]{2,1,0:T(8,128)S(1)}, f32[16,6,256]{2,1,0:T(8,128)S(1)}, u32[]{:S(2)}, u32[]{:S(2)}) collective-permute-start(f32[16,6,256]{2,1,0:T(8,128)S(1)} %get-tuple-element.10), channel_id=1, source_target_pairs={{1,0},{2,1},{3,2},{4,3},{5,4},{6,5},{7,6},{8,7},{9,8},{10,9},{11,1... | collective-permute-start | bytes 294920 | tf_op jit(solution)/shard_map/ppermute | solution.py:24
  26.8 0.7 pad_add_fusion.sc_ref
  27.5 1.0 collective-permute-done.ylo_ref
  28.5 8.4 %collective-permute-done.1.yhi_ref = f32[16,6,256]{2,1,0:T(8,128)S(1)} collective-permute-done((f32[16,6,256]{2,1,0:T(8,128)S(1)}, f32[16,6,256]{2,1,0:T(8,128)S(1)}, u32[]{:S(2)}, u32[]{:S(2)}) %collective-permute-start.1) | collective-permute-done | bytes 98336 | tf_op jit(solution)/shard_map/ppermute | solution.py:24
  36.9 2.6 %collective-permute-start.4 = (f32[2,6,12,256]{3,2,1,0:T(8,128)S(1)}, f32[2,6,12,256]{3,2,1,0:T(8,128)}, u32[]{:S(2)}, u32[]{:S(2)}) collective-permute-start(f32[2,6,12,256]{3,2,1,0:T(8,128)S(1)} %get-tuple-element.15), channel_id=1, source_target_pairs={{0,32},{32,64},{64,96},{1,33},{33,65},{65,97},{2,34},{34,66},{66,9... | collective-permute-start | bytes 442376 | tf_op jit(solution)/shard_map/ppermute | solution.py:24
  39.5 1.3 %collective-permute-start.5 = (f32[2,6,12,256]{3,2,1,0:T(8,128)S(1)}, f32[2,6,12,256]{3,2,1,0:T(8,128)}, u32[]{:S(2)}, u32[]{:S(2)}) collective-permute-start(f32[2,6,12,256]{3,2,1,0:T(8,128)S(1)} %get-tuple-element.14), channel_id=1, source_target_pairs={{32,0},{64,32},{96,64},{33,1},{65,33},{97,65},{34,2},{66,34},{98,6... | collective-permute-start | bytes 442376 | tf_op jit(solution)/shard_map/ppermute | solution.py:24
  40.8 1.0 copy.28
  41.8 16.3 %all-gather.3.cloned.1.call-done = f32[8,128,256]{2,1,0:T(8,128)} async-done(((f32[2,128,256]{2,1,0:T(8,128)}), f32[8,128,256]{2,1,0:T(8,128)}) %all-gather.3.cloned.1.call-update) | async-done | bytes 1048592 | tf_op jit(solution)/shard_map/all_gather | solution.py:188
  58.2 0.9 fusion.10
  59.0 4.7 %collective-permute-start.6 = (f32[8,6,256]{2,1,0:T(8,128)S(1)}, f32[8,6,256]{2,1,0:T(8,128)S(1)}, u32[]{:S(2)}, u32[]{:S(2)}) collective-permute-start(f32[8,6,256]{2,1,0:T(8,128)S(1)} %get-tuple-element.13), channel_id=1, source_target_pairs={{0,1},{1,2},{2,3},{3,4},{4,5},{5,6},{6,7},{7,8},{8,9},{9,10},{10,1... | collective-permute-start | bytes 147464 | tf_op jit(solution)/shard_map/ppermute | solution.py:24
  63.8 1.9 %collective-permute-start.7 = (f32[8,6,256]{2,1,0:T(8,128)S(1)}, f32[8,6,256]{2,1,0:T(8,128)S(1)}, u32[]{:S(2)}, u32[]{:S(2)}) collective-permute-start(f32[8,6,256]{2,1,0:T(8,128)S(1)} %get-tuple-element.12), channel_id=1, source_target_pairs={{1,0},{2,1},{3,2},{4,3},{5,4},{6,5},{7,6},{8,7},{9,8},{10,9},{11,1... | collective-permute-start | bytes 147464 | tf_op jit(solution)/shard_map/ppermute | solution.py:24
  65.8 0.8 copy.30
  66.6 7.0 %collective-permute-done.7.dhi_ref = f32[8,6,256]{2,1,0:T(8,128)S(1)} collective-permute-done((f32[8,6,256]{2,1,0:T(8,128)S(1)}, f32[8,6,256]{2,1,0:T(8,128)S(1)}, u32[]{:S(2)}, u32[]{:S(2)}) %collective-permute-start.7) | collective-permute-done | bytes 49184 | tf_op jit(solution)/shard_map/ppermute | solution.py:24
  73.6 0.6 copy-done.8
  74.2 27.6 %shard_map.86 = f32[8,128,256]{2,1,0:T(8,128)} custom-call(s32[6]{0:T(128)} %pad_add_fusion.sc_ref, f32[8]{0:T(128)} %ctab_ref.1, f32[8]{0:T(128)} %htab_ref.1, f32[2,8,128,256]{3,2,1,0:T(8,128)} %copy-done, f32[16,6,256]{2,1,0:T(8,128)} %copy-done.3, f32[16,6,256]{2,1,0:T(8,128)} %copy-done.4, f32[2,6,128,256]{3,2,1,0:T(8,128)} %collective-permute-done.2.xb_ref, ...), custom_call_target="tpu_custom_call" | custom-call | tf_op jit(solution)/shard_map/pallas_call | solution.py:206
  101.8 2.5 %copy.29 = f32[8,1,256,128]{3,2,1,0:T(8,128)} copy(f32[8,1,256,128]{2,3,0,1:T(8,128)} %bitcast.35) | data formatting | bytes 2097152
  (38 shorter events, 1.3 us)
Async XLA Ops:
  7.2 33.7 %reduce-scatter.2.cloned.1.call-start = ((), (), s32[]{:S(2)}) async-start(), calls=%async_computation.1 | async-start | bytes 655360 | tf_op jit(solution)/shard_map/reduce_scatter | solution.py:175
  7.2 3.4 %copy-start.5 = (f32[1,1,256,128]{3,2,1,0:T(8,128)S(1)}, f32[1,1,256,128]{3,2,1,0:T(8,128)}, u32[]{:S(2)}) copy-start(f32[1,1,256,128]{3,2,1,0:T(8,128)} %param.12) | copy-start | bytes 393220
  7.2 3.5 %copy-start.6 = (f32[1,1,256,128]{3,2,1,0:T(8,128)S(1)}, f32[1,1,256,128]{3,2,1,0:T(8,128)}, u32[]{:S(2)}) copy-start(f32[1,1,256,128]{3,2,1,0:T(8,128)} %param.11) | copy-start | bytes 393220
  9.7 1.9 %copy-start.1 = (f32[8,1,256,128]{3,2,1,0:T(8,128)S(1)}, f32[8,1,256,128]{3,2,1,0:T(8,128)}, u32[]{:S(2)}) copy-start(f32[8,1,256,128]{3,2,1,0:T(8,128)} %param.7) | copy-start | bytes 3145732
  10.6 47.6 %all-gather.3.cloned.1.call-start = ((), (), s32[]{:S(2)}) async-start(), calls=%async_computation.2 | async-start | bytes 1310720 | tf_op jit(solution)/shard_map/all_gather | solution.py:188
  10.7 1.4 %copy-start.2 = (s32[8,1,256,128]{3,2,1,0:T(8,128)S(1)}, s32[8,1,256,128]{3,2,1,0:T(8,128)}, u32[]{:S(2)}) copy-start(s32[8,1,256,128]{3,2,1,0:T(8,128)} %param.8) | copy-start | bytes 3145732
  14.6 51.9 %collective-permute-start.2 = (f32[2,6,128,256]{3,2,1,0:T(8,128)}, f32[2,6,128,256]{3,2,1,0:T(8,128)}, u32[]{:S(2)}, u32[]{:S(2)}) collective-permute-start(f32[2,6,128,256]{3,2,1,0:T(8,128)} %get-tuple-element.9), channel_id=1, source_target_pairs={{0,32},{32,64},{64,96},{1,33},{33,65},{65,97},{2,34},{34,66},{66,9... | collective-permute-start | bytes 4718600 | tf_op jit(solution)/shard_map/ppermute | solution.py:24
  17.5 9.3 %copy-start.9 = (s32[4]{0:T(128)S(1)}, s32[4]{0:T(128)}, u32[]{:S(2)}) copy-start(s32[4]{0:T(128)} %param.13) | copy-start | bytes 52
  17.5 49.0 %collective-permute-start.3 = (f32[2,6,128,256]{3,2,1,0:T(8,128)}, f32[2,6,128,256]{3,2,1,0:T(8,128)}, u32[]{:S(2)}, u32[]{:S(2)}) collective-permute-start(f32[2,6,128,256]{3,2,1,0:T(8,128)} %get-tuple-element.8), channel_id=1, source_target_pairs={{32,0},{64,32},{96,64},{33,1},{65,33},{97,65},{34,2},{66,34},{98,6... | collective-permute-start | bytes 4718600 | tf_op jit(solution)/shard_map/ppermute | solution.py:24
  19.1 54.5 %copy-start = (f32[2,8,128,256]{3,2,1,0:T(8,128)}, f32[2,8,128,256]{3,2,1,0:T(8,128)S(1)}, u32[]{:S(2)}) copy-start(f32[2,8,128,256]{3,2,1,0:T(8,128)S(1)} %pad_maximum_fusion.xc_ref) | copy-start | bytes 6291460
  19.2 9.3 %collective-permute-start = (f32[16,6,256]{2,1,0:T(8,128)S(1)}, f32[16,6,256]{2,1,0:T(8,128)S(1)}, u32[]{:S(2)}, u32[]{:S(2)}) collective-permute-start(f32[16,6,256]{2,1,0:T(8,128)S(1)} %get-tuple-element.11), channel_id=1, source_target_pairs={{0,1},{1,2},{2,3},{3,4},{4,5},{5,6},{6,7},{7,8},{8,9},{9,10},{10,1... | collective-permute-start | bytes 294920 | tf_op jit(solution)/shard_map/ppermute | solution.py:24
  24.9 11.9 %collective-permute-start.1 = (f32[16,6,256]{2,1,0:T(8,128)S(1)}, f32[16,6,256]{2,1,0:T(8,128)S(1)}, u32[]{:S(2)}, u32[]{:S(2)}) collective-permute-start(f32[16,6,256]{2,1,0:T(8,128)S(1)} %get-tuple-element.10), channel_id=1, source_target_pairs={{1,0},{2,1},{3,2},{4,3},{5,4},{6,5},{7,6},{8,7},{9,8},{10,9},{11,1... | collective-permute-start | bytes 294920 | tf_op jit(solution)/shard_map/ppermute | solution.py:24
  28.5 45.1 %copy-start.3 = (f32[16,6,256]{2,1,0:T(8,128)}, f32[16,6,256]{2,1,0:T(8,128)S(1)}, u32[]{:S(2)}) copy-start(f32[16,6,256]{2,1,0:T(8,128)S(1)} %collective-permute-done.ylo_ref) | copy-start | bytes 294916
  36.8 36.8 %copy-start.4 = (f32[16,6,256]{2,1,0:T(8,128)}, f32[16,6,256]{2,1,0:T(8,128)S(1)}, u32[]{:S(2)}) copy-start(f32[16,6,256]{2,1,0:T(8,128)S(1)} %collective-permute-done.1.yhi_ref) | copy-start | bytes 294916
  36.9 26.9 %collective-permute-start.4 = (f32[2,6,12,256]{3,2,1,0:T(8,128)S(1)}, f32[2,6,12,256]{3,2,1,0:T(8,128)}, u32[]{:S(2)}, u32[]{:S(2)}) collective-permute-start(f32[2,6,12,256]{3,2,1,0:T(8,128)S(1)} %get-tuple-element.15), channel_id=1, source_target_pairs={{0,32},{32,64},{64,96},{1,33},{33,65},{65,97},{2,34},{34,66},{66,9... | collective-permute-start | bytes 442376 | tf_op jit(solution)/shard_map/ppermute | solution.py:24
  39.5 27.0 %collective-permute-start.5 = (f32[2,6,12,256]{3,2,1,0:T(8,128)S(1)}, f32[2,6,12,256]{3,2,1,0:T(8,128)}, u32[]{:S(2)}, u32[]{:S(2)}) collective-permute-start(f32[2,6,12,256]{3,2,1,0:T(8,128)S(1)} %get-tuple-element.14), channel_id=1, source_target_pairs={{32,0},{64,32},{96,64},{33,1},{65,33},{97,65},{34,2},{66,34},{98,6... | collective-permute-start | bytes 442376 | tf_op jit(solution)/shard_map/ppermute | solution.py:24
  59.0 7.5 %collective-permute-start.6 = (f32[8,6,256]{2,1,0:T(8,128)S(1)}, f32[8,6,256]{2,1,0:T(8,128)S(1)}, u32[]{:S(2)}, u32[]{:S(2)}) collective-permute-start(f32[8,6,256]{2,1,0:T(8,128)S(1)} %get-tuple-element.13), channel_id=1, source_target_pairs={{0,1},{1,2},{2,3},{3,4},{4,5},{5,6},{6,7},{7,8},{8,9},{9,10},{10,1... | collective-permute-start | bytes 147464 | tf_op jit(solution)/shard_map/ppermute | solution.py:24
  63.8 9.8 %collective-permute-start.7 = (f32[8,6,256]{2,1,0:T(8,128)S(1)}, f32[8,6,256]{2,1,0:T(8,128)S(1)}, u32[]{:S(2)}, u32[]{:S(2)}) collective-permute-start(f32[8,6,256]{2,1,0:T(8,128)S(1)} %get-tuple-element.12), channel_id=1, source_target_pairs={{1,0},{2,1},{3,2},{4,3},{5,4},{6,5},{7,6},{8,7},{9,8},{10,9},{11,1... | collective-permute-start | bytes 147464 | tf_op jit(solution)/shard_map/ppermute | solution.py:24
  66.5 7.0 %copy-start.7 = (f32[8,6,256]{2,1,0:T(8,128)}, f32[8,6,256]{2,1,0:T(8,128)S(1)}, u32[]{:S(2)}) copy-start(f32[8,6,256]{2,1,0:T(8,128)S(1)} %collective-permute-done.6.dlo_ref) | copy-start | bytes 147460
  73.6 0.6 copy-start.8
Sparse Core Ops, SparseCore 0:
  10.9 21.4 reduce-scatter.1
  34.1 24.0 all-gather.2

commit v2 on v1

--- a/solution.py
+++ b/solution.py
@@ -37,8 +37,7 @@
 
 
 def sweep_kernel(nz, ny_total, local_depth, strip,
-                 sc_ref, ctab_ref, htab_ref, xc_ref, ylo_ref, yhi_ref, xb_ref, xa_ref,
-                 cb_ref, ca_ref, dc_ref, dlo_ref, dhi_ref,
+                 sc_ref, ctab_ref, htab_ref, xc_ref, xb_ref, xa_ref, dc_ref, ylo_ref, yhi_ref,
                  out_ref, t_s, cond_s, rhs_s, inv_s, gz_s, gx_s, gxl_s, gy_s, gyu_s, dl_s):
     ze = t_s.shape[1]
     ye = t_s.shape[2]
@@ -76,7 +75,8 @@
         rhs_s[l] = hval * temp
 
     def below(i, c):
-        tables(i, [(xb_ref[f, i], cb_ref[f, i, :HALO], cb_ref[f, i, HALO:]) for f in range(2)])
+        tables(i, [(xb_ref[f, i], ylo_ref[2 * local_depth + f * HALO + i],
+                    yhi_ref[2 * local_depth + f * HALO + i]) for f in range(2)])
         return c
 
     def centre(i, c):
@@ -86,21 +86,24 @@
 
     def above(i, c):
         tables(HALO + local_depth + i,
-               [(xa_ref[f, i], ca_ref[f, i, :HALO], ca_ref[f, i, HALO:]) for f in range(2)])
+               [(xa_ref[f, i], ylo_ref[2 * local_depth + (2 + f) * HALO + i],
+                 yhi_ref[2 * local_depth + (2 + f) * HALO + i]) for f in range(2)])
         return c
 
     lax.fori_loop(0, HALO, below, 0)
     lax.fori_loop(0, local_depth, centre, 0)
     lax.fori_loop(0, HALO, above, 0)
 
-    for d in range(dc_ref.shape[0]):
-        rel = sc_ref[2 + d] - z0
+    dies = dc_ref.shape[0]
+    dl_row = 2 * local_depth + 4 * HALO
+    for o in range(dies):
+        rel = sc_ref[2 + (g + dies - o) % dies] - z0
         relc = jnp.clip(rel, 0, ze - 1)
 
         @pl.when((rel >= 0) & (rel < ze))
         def _():
             for f in range(2):
-                put(dl_s.at[f], dc_ref[d, f], dlo_ref[2 * d + f], dhi_ref[2 * d + f])
+                put(dl_s.at[f], dc_ref[o, f], ylo_ref[dl_row + 2 * o + f], yhi_ref[dl_row + 2 * o + f])
             power = dl_s[0] + dl_s[1] * jnp.exp(LEAK_SLOPE * t_s[0, relc])
             rhs_s[relc] = inv_s[relc] * t_s[0, relc] + power
 
@@ -164,37 +167,40 @@
     local_depth, nx, strip = temp_start.shape
     depth_n = lax.axis_size("depth")
     lat_n = lax.axis_size("lat")
+    dies = dyn_power.shape[0] * depth_n
     nz = local_depth * depth_n
     g = lax.axis_index("depth")
     s = lax.axis_index("lat")
     first_layer = g * local_depth
-    layer_ids = first_layer + lax.iota(jnp.int32, local_depth)
-
-    select = (die_layer[:, None] == layer_ids[None, :]).astype(jnp.float32)
-    picked = jnp.einsum("dz,zxy->dxy", select, temp_start, precision=lax.Precision.HIGHEST)
-    die_temp = lax.psum_scatter(picked, "depth", scatter_dimension=0, tiled=True)
-    die_power = dyn_power[:, 0] + leak_ref[:, 0] * jnp.exp(LEAK_SLOPE * die_temp)
 
     tt = jnp.transpose(temp_start, (0, 2, 1))
     mt = jnp.transpose(cells_mat, (0, 2, 1)).astype(jnp.float32)
     tm = jnp.stack([tt, mt])
     dl = jnp.transpose(jnp.concatenate([dyn_power[:, 0], leak_ref[:, 0]]), (0, 2, 1))
 
+    def pick(die):
+        at = die_layer[die] - first_layer
+        layer = lax.dynamic_index_in_dim(tt, jnp.clip(at, 0, local_depth - 1), 0, keepdims=True)
+        return jnp.where((at >= 0) & (at < local_depth), layer, 0.0)
+
     xb = from_behind(tm[:, local_depth - HALO:], "depth", 1)
     xa = from_behind(tm[:, :HALO], "depth", -1)
-    rows = tm.reshape(2 * local_depth, strip, nx)
-    ylo = from_behind(rows[:, strip - HALO:], "lat", 1)
-    yhi = from_behind(rows[:, :HALO], "lat", -1)
-    dc = lax.all_gather(dl, "depth", axis=0, tiled=False)
-
-    ylo2 = ylo.reshape(2, local_depth, HALO, nx)
-    yhi2 = yhi.reshape(2, local_depth, HALO, nx)
-    side = jnp.concatenate([ylo2, yhi2], axis=2)
-    cb = from_behind(side[:, local_depth - HALO:], "depth", 1)
-    ca = from_behind(side[:, :HALO], "depth", -1)
-    drows = dc.reshape(-1, strip, nx)
-    dlo = from_behind(drows[:, strip - HALO:], "lat", 1)
-    dhi = from_behind(drows[:, :HALO], "lat", -1)
+    slots = [dl]
+    die_temp = pick(g)
+    for o in range(1, dies):
+        route = [(i, (i + o) % depth_n) for i in range(depth_n)]
+        sent = jnp.concatenate([dl, pick((g + o) % dies)])
+        got = lax.ppermute(sent, "depth", route)
+        slots.append(got[:2])
+        die_temp = die_temp + got[2:]
+    dc = jnp.stack(slots)
+    die_temp = jnp.transpose(die_temp, (0, 2, 1))
+    die_power = dyn_power[:, 0] + leak_ref[:, 0] * jnp.exp(LEAK_SLOPE * die_temp)
+
+    held = [tm.reshape(-1, strip, nx), xb.reshape(-1, strip, nx), xa.reshape(-1, strip, nx),
+            dc.reshape(-1, strip, nx)]
+    ylo = from_behind(jnp.concatenate([h[:, strip - HALO:] for h in held]), "lat", 1)
+    yhi = from_behind(jnp.concatenate([h[:, :HALO] for h in held]), "lat", -1)
 
     sc = jnp.concatenate([jnp.stack([g, s]).astype(jnp.int32), die_layer.astype(jnp.int32)])
     ze = local_depth + 2 * HALO
@@ -206,13 +212,13 @@
     out = pl.pallas_call(
         kern,
         out_shape=jax.ShapeDtypeStruct((local_depth, strip, nx), jnp.float32),
-        in_specs=[smem] * 3 + [vmem] * 10,
+        in_specs=[smem] * 3 + [vmem] * 6,
         out_specs=vmem,
         scratch_shapes=([pltpu.VMEM((2,) + full, jnp.float32)] + [pltpu.VMEM(full, jnp.float32)] * 8
                         + [pltpu.VMEM((2, ye, nx), jnp.float32)]),
         compiler_params=pltpu.CompilerParams(vmem_limit_bytes=60 * 1024 * 1024),
         interpret=INTERPRET,
-    )(sc, conduct_table, capacity_table, tm, ylo, yhi, xb, xa, cb, ca, dc, dlo, dhi)
+    )(sc, conduct_table, capacity_table, tm, xb, xa, dc, ylo, yhi)
     temp_new = jnp.transpose(out, (0, 2, 1))
     return (temp_new[:, None], die_power[:, None])
 

time: 112 us -> 100 us (0.89)
  the two profiles are of different devices: /device:TPU:14 before, /device:TPU:38 now
where the time goes in v2:
time: 100 us; the launch traced here: 99.7 us
  waiting for transfers between devices  35.5 us (36%)
  Pallas kernels  27.5 us (28%)
  starting transfers between devices  13.5 us (14%)
  local copies, waits for them, and re-layouts  12.5 us (12%)
  other arithmetic  7.03 us (7%)
  between operations  3.63 us (4%)
    pallas_call x1, Pallas kernels, local(): pl.pallas_call(kern, out_shape=jax.ShapeDtypeStruct((local_depth, strip,...  27.5 us
    ppermute x3, waiting for transfers between devices, local(): got = lax.ppermute(sent, 'depth', route)  22.2 us
    ppermute x4, waiting for transfers between devices, from_behind(): return lax.ppermute(block, axis, route)  13.3 us
    ppermute x4, starting transfers between devices, from_behind(): return lax.ppermute(block, axis, route)  10.5 us
    unnamed x30, local copies, waits for them, and re-layouts  6.67 us
    ppermute x3, starting transfers between devices, local(): got = lax.ppermute(sent, 'depth', route)  2.92 us
    another operation x3, local copies, waits for them, and re-layouts, local(): dc = jnp.stack(slots)  2.9 us
    another operation x3, other arithmetic, local(): tm = jnp.stack([tt, mt])  2.27 us
  transfers between devices with their start and end apart: 7, of which 6 were waited for; matrix products, arithmetic and copies ran while one was open for 11% of the time, Pallas kernels for 0%

profile of v2, /device:TPU:38, one launch (start us, length us, event | category | flops | bytes accessed | tf_op | source)
XLA Modules:
  0.0 99.7 jit_solution(15498061788091093848)
XLA Ops:
  0.6 1.6 %copy.10 = s32[8,1,256,128]{2,3,0,1:T(8,128)S(1)} copy(s32[8,1,256,128]{3,2,1,0:T(8,128)} %param.8) | data formatting | bytes 2097152 | tf_op args[1]
  2.8 2.0 %fusion.1 = (f32[2,6,128,256]{3,2,1,0:T(8,128)}, f32[2,6,128,256]{3,2,1,0:T(8,128)}) fusion(f32[1,8,128,256]{3,2,1,0:T(8,128)S(1)} %bitcast.66, f32[1,8,128,256]{3,2,1,0:T(8,128)S(1)} %convert_bitcast_fusion), kind=kLoop, calls=%fused_computation.6 | loop fusion | flops 786432 | bytes 5242880 | tf_op jit(solution)/shard_map/stack | solution.py:178
  4.8 1.9 %collective-permute-start.1 = (f32[2,6,128,256]{3,2,1,0:T(8,128)}, f32[2,6,128,256]{3,2,1,0:T(8,128)}, u32[]{:S(2)}, u32[]{:S(2)}) collective-permute-start(f32[2,6,128,256]{3,2,1,0:T(8,128)} %get-tuple-element.6), channel_id=1, source_target_pairs={{32,0},{64,32},{96,64},{33,1},{65,33},{97,65},{34,2},{66,34},{98,6... | collective-permute-start | bytes 4718600 | tf_op jit(solution)/shard_map/ppermute | solution.py:24
  11.5 1.1 %pad_maximum_fusion.4 = (f32[3,128,256]{2,1,0:T(8,128)}, f32[3,128,256]{2,1,0:T(8,128)}, f32[3,128,256]{2,1,0:T(8,128)}) fusion(f32[2,128,256]{2,1,0:T(8,128)S(1)} %get-tuple-element.19, f32[1,128,256]{2,1,0:T(8,128)S(1)} %select_bitcast_fusion.2, f32[1,128,256]{2,1,0:T(8,128)S(1)} %get-tuple-element.28, f32[1,128,256]{2,1,0:T(8,128)S(1)} %get-tuple-element.27), kind=kLoop, calls=%fused_computation.11 | loop fusion | flops 294912 | bytes 1835008 | tf_op jit(solution)/shard_map/concatenate | solution.py:192
  12.6 1.6 %collective-permute-start.2 = (f32[3,128,256]{2,1,0:T(8,128)}, f32[3,128,256]{2,1,0:T(8,128)}, u32[]{:S(2)}, u32[]{:S(2)}) collective-permute-start(f32[3,128,256]{2,1,0:T(8,128)} %get-tuple-element.20), channel_id=1, source_target_pairs={{0,32},{32,64},{64,96},{96,0},{1,33},{33,65},{65,97},{97,1},{2,34}... | collective-permute-start | bytes 1179656 | tf_op jit(solution)/shard_map/ppermute | solution.py:193
  14.2 1.4 %collective-permute-start.4 = (f32[3,128,256]{2,1,0:T(8,128)}, f32[3,128,256]{2,1,0:T(8,128)}, u32[]{:S(2)}, u32[]{:S(2)}) collective-permute-start(f32[3,128,256]{2,1,0:T(8,128)} %get-tuple-element.22), channel_id=1, source_target_pairs={{0,96},{32,0},{64,32},{96,64},{1,97},{33,1},{65,33},{97,65},{2,98}... | collective-permute-start | bytes 1179656 | tf_op jit(solution)/shard_map/ppermute | solution.py:193
  15.6 1.9 %collective-permute-start = (f32[2,6,128,256]{3,2,1,0:T(8,128)}, f32[2,6,128,256]{3,2,1,0:T(8,128)}, u32[]{:S(2)}, u32[]{:S(2)}) collective-permute-start(f32[2,6,128,256]{3,2,1,0:T(8,128)} %get-tuple-element.7), channel_id=1, source_target_pairs={{0,32},{32,64},{64,96},{1,33},{33,65},{65,97},{2,34},{34,66},{66,9... | collective-permute-start | bytes 4718600 | tf_op jit(solution)/shard_map/ppermute | solution.py:24
  17.7 4.5 %collective-permute-done.2 = f32[3,128,256]{2,1,0:T(8,128)} collective-permute-done((f32[3,128,256]{2,1,0:T(8,128)}, f32[3,128,256]{2,1,0:T(8,128)}, u32[]{:S(2)}, u32[]{:S(2)}) %collective-permute-start.2) | collective-permute-done | bytes 393248 | tf_op jit(solution)/shard_map/ppermute | solution.py:193
  22.2 1.0 slice_bitcast_fusion.2
  23.2 14.4 %collective-permute-done.3 = f32[3,128,256]{2,1,0:T(8,128)} collective-permute-done((f32[3,128,256]{2,1,0:T(8,128)}, f32[3,128,256]{2,1,0:T(8,128)}, u32[]{:S(2)}, u32[]{:S(2)}) %collective-permute-start.3) | collective-permute-done | bytes 393248 | tf_op jit(solution)/shard_map/ppermute | solution.py:193
  37.6 1.0 slice_bitcast_fusion.1
  38.6 3.2 %collective-permute-done.4 = f32[3,128,256]{2,1,0:T(8,128)} collective-permute-done((f32[3,128,256]{2,1,0:T(8,128)}, f32[3,128,256]{2,1,0:T(8,128)}, u32[]{:S(2)}, u32[]{:S(2)}) %collective-permute-start.4) | collective-permute-done | bytes 393248 | tf_op jit(solution)/shard_map/ppermute | solution.py:193
  41.8 1.0 slice_bitcast_fusion
  42.8 1.1 %pad_maximum_fusion.1.dc_ref = f32[4,2,128,256]{3,2,1,0:T(8,128)S(1)} fusion(f32[1,2,128,256]{3,2,1,0:T(8,128)S(1)} %slice_bitcast_fusion, f32[1,2,128,256]{3,2,1,0:T(8,128)S(1)} %slice_bitcast_fusion.1, f32[1,2,128,256]{3,2,1,0:T(8,128)S(1)} %slice_bitcast_fusion.2, f32[1,2,128,256]{3,2,1,0:T(8,128)} %get-tuple-element.18), kind=kLoop, calls=%fused_computation.7 | loop fusion | flops 786432 | bytes 2097152 | tf_op jit(solution)/shard_map/stack | solution.py:196
  43.9 1.2 %fusion.12 = (f32[12,6,256]{2,1,0:T(8,128)S(1)}, f32[12,6,256]{2,1,0:T(8,128)S(1)}) fusion(f32[12,128,256]{2,1,0:T(8,128)} %bitcast.26), kind=kLoop, calls=%fused_computation.39 | loop fusion | bytes 294912 | tf_op jit(solution)/shard_map/slice | solution.py:203
  45.1 4.5 %collective-permute-done.xb_ref = f32[2,6,128,256]{3,2,1,0:T(8,128)} collective-permute-done((f32[2,6,128,256]{3,2,1,0:T(8,128)}, f32[2,6,128,256]{3,2,1,0:T(8,128)}, u32[]{:S(2)}, u32[]{:S(2)}) %collective-permute-start) | collective-permute-done | bytes 1572896 | tf_op jit(solution)/shard_map/ppermute | solution.py:24
  49.6 1.0 fusion.11
  50.7 4.8 %collective-permute-start.5 = (f32[48,6,256]{2,1,0:T(8,128)S(1)}, f32[48,6,256]{2,1,0:T(8,128)S(1)}, u32[]{:S(2)}, u32[]{:S(2)}) collective-permute-start(f32[48,6,256]{2,1,0:T(8,128)S(1)} %pad_maximum_fusion.5), channel_id=1, source_target_pairs={{0,1},{1,2},{2,3},{3,4},{4,5},{5,6},{6,7},{7,8},{8,9},{9,10},{10,1... | collective-permute-start | bytes 884744 | tf_op jit(solution)/shard_map/ppermute | solution.py:24
  55.5 1.9 %collective-permute-start.6 = (f32[48,6,256]{2,1,0:T(8,128)S(1)}, f32[48,6,256]{2,1,0:T(8,128)S(1)}, u32[]{:S(2)}, u32[]{:S(2)}) collective-permute-start(f32[48,6,256]{2,1,0:T(8,128)S(1)} %pad_maximum_fusion.6), channel_id=1, source_target_pairs={{1,0},{2,1},{3,2},{4,3},{5,4},{6,5},{7,6},{8,7},{9,8},{10,9},{11,1... | collective-permute-start | bytes 884744 | tf_op jit(solution)/shard_map/ppermute | solution.py:24
  58.2 1.1 %fusion.9 = f32[1,1,256,128]{2,3,1,0:T(8,128)S(1)} fusion(f32[3,128,256]{2,1,0:T(8,128)} %collective-permute-done.4, f32[3,128,256]{2,1,0:T(8,128)} %collective-permute-done.3, f32[3,128,256]{2,1,0:T(8,128)} %collective-permute-done.2, f32[1,1,256,128]{2,3,1,0:T(8,128)S(1)} %copy.22, pred[]{:T(512)S(6)} %and.33, f32[1,1,256,128]{2,3,1,0:T(8,128)S(1)} %copy.12, ...), kind=kLoop, calls=%fused_computation.26 | loop fusion | flops 229376 | bytes 917505 | tf_op jit(solution)/shard_map/broadcast_in_dim | solution.py:223
  60.7 8.1 %collective-permute-done.6.yhi_ref = f32[48,6,256]{2,1,0:T(8,128)S(1)} collective-permute-done((f32[48,6,256]{2,1,0:T(8,128)S(1)}, f32[48,6,256]{2,1,0:T(8,128)S(1)}, u32[]{:S(2)}, u32[]{:S(2)}) %collective-permute-start.6) | collective-permute-done | bytes 294944 | tf_op jit(solution)/shard_map/ppermute | solution.py:24
  68.8 0.8 copy-done.6
  69.6 27.5 %shard_map.86 = f32[8,128,256]{2,1,0:T(8,128)} custom-call(s32[6]{0:T(128)} %pad_add_fusion.sc_ref, f32[8]{0:T(128)} %ctab_ref.1, f32[8]{0:T(128)} %htab_ref.1, f32[2,8,128,256]{3,2,1,0:T(8,128)} %copy-done, f32[2,6,128,256]{3,2,1,0:T(8,128)} %collective-permute-done.xb_ref, f32[2,6,128,256]{3,2,1,0:T(8,128)} %collective-permute-done.1.xa_ref, ...), custom_call_target="tpu_custom_call" | custom-call | tf_op jit(solution)/shard_map/pallas_call | solution.py:212
  97.1 2.5 %copy.17 = f32[8,1,256,128]{3,2,1,0:T(8,128)} copy(f32[8,1,256,128]{2,3,0,1:T(8,128)} %bitcast.69) | data formatting | bytes 2097152
  (42 shorter events, 4.9 us)
Async XLA Ops:
  0.6 1.8 %copy-start.4 = (f32[8,1,256,128]{3,2,1,0:T(8,128)S(1)}, f32[8,1,256,128]{3,2,1,0:T(8,128)}, u32[]{:S(2)}) copy-start(f32[8,1,256,128]{3,2,1,0:T(8,128)} %param.7) | copy-start | bytes 3145732
  2.7 2.1 %copy-start.1 = (f32[8,1,256,128]{2,3,0,1:T(8,128)}, f32[8,1,256,128]{2,3,0,1:T(8,128)S(1)}, u32[]{:S(2)}) copy-start(f32[8,1,256,128]{2,3,0,1:T(8,128)S(1)} %copy.9) | copy-start | bytes 3145732
  2.8 4.0 %copy-start.9 = (s32[4]{0:T(128)S(1)}, s32[4]{0:T(128)}, u32[]{:S(2)}) copy-start(s32[4]{0:T(128)} %param.13) | copy-start | bytes 52
  2.8 7.3 %copy-start.7 = (f32[1,1,256,128]{3,2,1,0:T(8,128)S(1)}, f32[1,1,256,128]{3,2,1,0:T(8,128)}, u32[]{:S(2)}) copy-start(f32[1,1,256,128]{3,2,1,0:T(8,128)} %param.11) | copy-start | bytes 393220
  2.8 7.4 %copy-start.8 = (f32[1,1,256,128]{3,2,1,0:T(8,128)S(1)}, f32[1,1,256,128]{3,2,1,0:T(8,128)}, u32[]{:S(2)}) copy-start(f32[1,1,256,128]{3,2,1,0:T(8,128)} %param.12) | copy-start | bytes 393220
  4.8 39.1 %collective-permute-start.1 = (f32[2,6,128,256]{3,2,1,0:T(8,128)}, f32[2,6,128,256]{3,2,1,0:T(8,128)}, u32[]{:S(2)}, u32[]{:S(2)}) collective-permute-start(f32[2,6,128,256]{3,2,1,0:T(8,128)} %get-tuple-element.6), channel_id=1, source_target_pairs={{32,0},{64,32},{96,64},{33,1},{65,33},{97,65},{34,2},{66,34},{98,6... | collective-permute-start | bytes 4718600 | tf_op jit(solution)/shard_map/ppermute | solution.py:24
  10.7 6.8 %copy-start.2 = (f32[8,1,256,128]{2,3,0,1:T(8,128)S(1)}, f32[8,1,256,128]{2,3,0,1:T(8,128)}, u32[]{:S(2)}) copy-start(f32[8,1,256,128]{2,3,0,1:T(8,128)} %copy-done.1) | copy-start | bytes 3145732
  12.6 9.6 %collective-permute-start.2 = (f32[3,128,256]{2,1,0:T(8,128)}, f32[3,128,256]{2,1,0:T(8,128)}, u32[]{:S(2)}, u32[]{:S(2)}) collective-permute-start(f32[3,128,256]{2,1,0:T(8,128)} %get-tuple-element.20), channel_id=1, source_target_pairs={{0,32},{32,64},{64,96},{96,0},{1,33},{33,65},{65,97},{97,1},{2,34}... | collective-permute-start | bytes 1179656 | tf_op jit(solution)/shard_map/ppermute | solution.py:193
  14.2 23.4 %collective-permute-start.3 = (f32[3,128,256]{2,1,0:T(8,128)}, f32[3,128,256]{2,1,0:T(8,128)}, u32[]{:S(2)}, u32[]{:S(2)}) collective-permute-start(f32[3,128,256]{2,1,0:T(8,128)} %get-tuple-element.21), channel_id=1, source_target_pairs={{0,64},{32,96},{64,0},{96,32},{1,65},{33,97},{65,1},{97,33},{2,66}... | collective-permute-start | bytes 1179656 | tf_op jit(solution)/shard_map/ppermute | solution.py:193
  14.2 27.6 %collective-permute-start.4 = (f32[3,128,256]{2,1,0:T(8,128)}, f32[3,128,256]{2,1,0:T(8,128)}, u32[]{:S(2)}, u32[]{:S(2)}) collective-permute-start(f32[3,128,256]{2,1,0:T(8,128)} %get-tuple-element.22), channel_id=1, source_target_pairs={{0,96},{32,0},{64,32},{96,64},{1,97},{33,1},{65,33},{97,65},{2,98}... | collective-permute-start | bytes 1179656 | tf_op jit(solution)/shard_map/ppermute | solution.py:193
  15.6 34.1 %collective-permute-start = (f32[2,6,128,256]{3,2,1,0:T(8,128)}, f32[2,6,128,256]{3,2,1,0:T(8,128)}, u32[]{:S(2)}, u32[]{:S(2)}) collective-permute-start(f32[2,6,128,256]{3,2,1,0:T(8,128)} %get-tuple-element.7), channel_id=1, source_target_pairs={{0,32},{32,64},{64,96},{1,33},{33,65},{65,97},{2,34},{34,66},{66,9... | collective-permute-start | bytes 4718600 | tf_op jit(solution)/shard_map/ppermute | solution.py:24
  17.6 26.2 %copy-start = (f32[2,8,128,256]{3,2,1,0:T(8,128)}, f32[2,8,128,256]{3,2,1,0:T(8,128)S(1)}, u32[]{:S(2)}) copy-start(f32[2,8,128,256]{3,2,1,0:T(8,128)S(1)} %pad_maximum_fusion.xc_ref) | copy-start | bytes 6291460
  43.9 15.4 %copy-start.3 = (f32[4,2,128,256]{3,2,1,0:T(8,128)}, f32[4,2,128,256]{3,2,1,0:T(8,128)S(1)}, u32[]{:S(2)}) copy-start(f32[4,2,128,256]{3,2,1,0:T(8,128)S(1)} %pad_maximum_fusion.1.dc_ref) | copy-start | bytes 3145732
  50.7 10.1 %collective-permute-start.5 = (f32[48,6,256]{2,1,0:T(8,128)S(1)}, f32[48,6,256]{2,1,0:T(8,128)S(1)}, u32[]{:S(2)}, u32[]{:S(2)}) collective-permute-start(f32[48,6,256]{2,1,0:T(8,128)S(1)} %pad_maximum_fusion.5), channel_id=1, source_target_pairs={{0,1},{1,2},{2,3},{3,4},{4,5},{5,6},{6,7},{7,8},{8,9},{9,10},{10,1... | collective-permute-start | bytes 884744 | tf_op jit(solution)/shard_map/ppermute | solution.py:24
  55.5 13.3 %collective-permute-start.6 = (f32[48,6,256]{2,1,0:T(8,128)S(1)}, f32[48,6,256]{2,1,0:T(8,128)S(1)}, u32[]{:S(2)}, u32[]{:S(2)}) collective-permute-start(f32[48,6,256]{2,1,0:T(8,128)S(1)} %pad_maximum_fusion.6), channel_id=1, source_target_pairs={{1,0},{2,1},{3,2},{4,3},{5,4},{6,5},{7,6},{8,7},{9,8},{10,9},{11,1... | collective-permute-start | bytes 884744 | tf_op jit(solution)/shard_map/ppermute | solution.py:24
  60.7 8.1 %copy-start.5 = (f32[48,6,256]{2,1,0:T(8,128)}, f32[48,6,256]{2,1,0:T(8,128)S(1)}, u32[]{:S(2)}) copy-start(f32[48,6,256]{2,1,0:T(8,128)S(1)} %collective-permute-done.5.ylo_ref) | copy-start | bytes 884740
  68.8 0.8 copy-start.6

commit v3 on v2

--- a/solution.py
+++ b/solution.py
@@ -37,8 +37,9 @@
 
 
 def sweep_kernel(nz, ny_total, local_depth, strip,
-                 sc_ref, ctab_ref, htab_ref, xc_ref, xb_ref, xa_ref, dc_ref, ylo_ref, yhi_ref,
-                 out_ref, t_s, cond_s, rhs_s, inv_s, gz_s, gx_s, gxl_s, gy_s, gyu_s, dl_s):
+                 sc_ref, ctab_ref, htab_ref, tc_ref, mc_ref, tb_ref, mb_ref, ta_ref, ma_ref,
+                 ylo_ref, yhi_ref, cb_ref, ca_ref, dc_ref,
+                 out_ref, t_s, cond_s, rhs_s, inv_s, gz_s, gx_s, gxl_s, gy_s, gyu_s):
     ze = t_s.shape[1]
     ye = t_s.shape[2]
     xe = t_s.shape[3]
@@ -60,9 +61,9 @@
         dst[0:PAD_Y - HALO] = zlo
         dst[top:ye] = zhi
 
-    def tables(l, parts):
-        for f, dst in ((0, t_s.at[0, l]), (1, cond_s.at[l])):
-            put(dst, *parts[f])
+    def tables(l, temp_raw, mat_raw, t_lo, t_hi, m_lo, m_hi):
+        put(t_s.at[0, l], temp_raw.T, t_lo, t_hi)
+        put(cond_s.at[l], mat_raw.T.astype(jnp.float32), m_lo, m_hi)
         temp = t_s[0, l]
         mat = cond_s[l]
         zg = z0 + l
@@ -75,19 +76,18 @@
         rhs_s[l] = hval * temp
 
     def below(i, c):
-        tables(i, [(xb_ref[f, i], ylo_ref[2 * local_depth + f * HALO + i],
-                    yhi_ref[2 * local_depth + f * HALO + i]) for f in range(2)])
+        tables(i, tb_ref[i], mb_ref[i], cb_ref[0, i, :HALO], cb_ref[0, i, HALO:],
+               cb_ref[1, i, :HALO], cb_ref[1, i, HALO:])
         return c
 
     def centre(i, c):
-        tables(HALO + i, [(xc_ref[f, i], ylo_ref[f * local_depth + i], yhi_ref[f * local_depth + i])
-                          for f in range(2)])
+        tables(HALO + i, tc_ref[i], mc_ref[i], ylo_ref[i], yhi_ref[i],
+               ylo_ref[local_depth + i], yhi_ref[local_depth + i])
         return c
 
     def above(i, c):
-        tables(HALO + local_depth + i,
-               [(xa_ref[f, i], ylo_ref[2 * local_depth + (2 + f) * HALO + i],
-                 yhi_ref[2 * local_depth + (2 + f) * HALO + i]) for f in range(2)])
+        tables(HALO + local_depth + i, ta_ref[i], ma_ref[i], ca_ref[0, i, :HALO], ca_ref[0, i, HALO:],
+               ca_ref[1, i, :HALO], ca_ref[1, i, HALO:])
         return c
 
     lax.fori_loop(0, HALO, below, 0)
@@ -95,16 +95,13 @@
     lax.fori_loop(0, HALO, above, 0)
 
     dies = dc_ref.shape[0]
-    dl_row = 2 * local_depth + 4 * HALO
     for o in range(dies):
         rel = sc_ref[2 + (g + dies - o) % dies] - z0
         relc = jnp.clip(rel, 0, ze - 1)
 
         @pl.when((rel >= 0) & (rel < ze))
         def _():
-            for f in range(2):
-                put(dl_s.at[f], dc_ref[o, f], ylo_ref[dl_row + 2 * o + f], yhi_ref[dl_row + 2 * o + f])
-            power = dl_s[0] + dl_s[1] * jnp.exp(LEAK_SLOPE * t_s[0, relc])
+            power = dc_ref[o, 0] + dc_ref[o, 1] * jnp.exp(LEAK_SLOPE * t_s[0, relc])
             rhs_s[relc] = inv_s[relc] * t_s[0, relc] + power
 
     def faces_z(l, c):
@@ -155,7 +152,7 @@
 
     def final(i, c):
         new = relax(last, HALO + i)
-        out_ref[i] = new[PAD_Y:PAD_Y + strip]
+        out_ref[i] = new[PAD_Y:PAD_Y + strip].T
         return c
 
     lax.fori_loop(0, local_depth, final, 0)
@@ -173,54 +170,59 @@
     s = lax.axis_index("lat")
     first_layer = g * local_depth
 
-    tt = jnp.transpose(temp_start, (0, 2, 1))
-    mt = jnp.transpose(cells_mat, (0, 2, 1)).astype(jnp.float32)
-    tm = jnp.stack([tt, mt])
-    dl = jnp.transpose(jnp.concatenate([dyn_power[:, 0], leak_ref[:, 0]]), (0, 2, 1))
-
     def pick(die):
         at = die_layer[die] - first_layer
-        layer = lax.dynamic_index_in_dim(tt, jnp.clip(at, 0, local_depth - 1), 0, keepdims=True)
+        layer = lax.dynamic_index_in_dim(temp_start, jnp.clip(at, 0, local_depth - 1), 0, keepdims=True)
         return jnp.where((at >= 0) & (at < local_depth), layer, 0.0)
 
-    xb = from_behind(tm[:, local_depth - HALO:], "depth", 1)
-    xa = from_behind(tm[:, :HALO], "depth", -1)
-    slots = [dl]
+    tb = from_behind(temp_start[local_depth - HALO:], "depth", 1)
+    mb = from_behind(cells_mat[local_depth - HALO:], "depth", 1)
+    ta = from_behind(temp_start[:HALO], "depth", -1)
+    ma = from_behind(cells_mat[:HALO], "depth", -1)
     die_temp = pick(g)
     for o in range(1, dies):
         route = [(i, (i + o) % depth_n) for i in range(depth_n)]
-        sent = jnp.concatenate([dl, pick((g + o) % dies)])
-        got = lax.ppermute(sent, "depth", route)
-        slots.append(got[:2])
-        die_temp = die_temp + got[2:]
+        die_temp = die_temp + lax.ppermute(pick((g + o) % dies), "depth", route)
+    die_power = dyn_power[:, 0] + leak_ref[:, 0] * jnp.exp(LEAK_SLOPE * die_temp)
+
+    fields = jnp.concatenate([temp_start, cells_mat.astype(jnp.float32), dyn_power[:, 0], leak_ref[:, 0]])
+    nf = fields.shape[0]
+    last_cols = jnp.transpose(fields[:, :, strip - HALO:], (0, 2, 1))
+    first_cols = jnp.transpose(fields[:, :, :HALO], (0, 2, 1))
+    ylo = from_behind(last_cols, "lat", 1)
+    yhi = from_behind(first_cols, "lat", -1)
+
+    ye = PAD_Y + strip + HALO + (-(PAD_Y + strip + HALO)) % 8
+    side = jnp.concatenate([ylo[:2 * local_depth].reshape(2, local_depth, HALO, nx),
+                            yhi[:2 * local_depth].reshape(2, local_depth, HALO, nx)], axis=2)
+    cb = from_behind(side[:, local_depth - HALO:], "depth", 1)
+    ca = from_behind(side[:, :HALO], "depth", -1)
+    dl = jnp.concatenate([
+        jnp.zeros((2, PAD_Y - HALO, nx), jnp.float32), ylo[nf - 2:],
+        jnp.transpose(jnp.concatenate([dyn_power[:, 0], leak_ref[:, 0]]), (0, 2, 1)),
+        yhi[nf - 2:], jnp.zeros((2, ye - (PAD_Y + strip + HALO), nx), jnp.float32)], axis=1)
+    slots = [dl]
+    for o in range(1, dies):
+        route = [(i, (i + o) % depth_n) for i in range(depth_n)]
+        slots.append(lax.ppermute(dl, "depth", route))
     dc = jnp.stack(slots)
-    die_temp = jnp.transpose(die_temp, (0, 2, 1))
-    die_power = dyn_power[:, 0] + leak_ref[:, 0] * jnp.exp(LEAK_SLOPE * die_temp)
-
-    held = [tm.reshape(-1, strip, nx), xb.reshape(-1, strip, nx), xa.reshape(-1, strip, nx),
-            dc.reshape(-1, strip, nx)]
-    ylo = from_behind(jnp.concatenate([h[:, strip - HALO:] for h in held]), "lat", 1)
-    yhi = from_behind(jnp.concatenate([h[:, :HALO] for h in held]), "lat", -1)
 
     sc = jnp.concatenate([jnp.stack([g, s]).astype(jnp.int32), die_layer.astype(jnp.int32)])
     ze = local_depth + 2 * HALO
-    ye = PAD_Y + strip + HALO + (-(PAD_Y + strip + HALO)) % 8
     smem = pl.BlockSpec(memory_space=pltpu.MemorySpace.SMEM)
     vmem = pl.BlockSpec(memory_space=pltpu.MemorySpace.VMEM)
     full = (ze, ye, nx)
     kern = functools.partial(sweep_kernel, nz, strip * lat_n, local_depth, strip)
     out = pl.pallas_call(
         kern,
-        out_shape=jax.ShapeDtypeStruct((local_depth, strip, nx), jnp.float32),
-        in_specs=[smem] * 3 + [vmem] * 6,
+        out_shape=jax.ShapeDtypeStruct((local_depth, nx, strip), jnp.float32),
+        in_specs=[smem] * 3 + [vmem] * 11,
         out_specs=vmem,
-        scratch_shapes=([pltpu.VMEM((2,) + full, jnp.float32)] + [pltpu.VMEM(full, jnp.float32)] * 8
-                        + [pltpu.VMEM((2, ye, nx), jnp.float32)]),
+        scratch_shapes=([pltpu.VMEM((2,) + full, jnp.float32)] + [pltpu.VMEM(full, jnp.float32)] * 8),
         compiler_params=pltpu.CompilerParams(vmem_limit_bytes=60 * 1024 * 1024),
         interpret=INTERPRET,
-    )(sc, conduct_table, capacity_table, tm, xb, xa, dc, ylo, yhi)
-    temp_new = jnp.transpose(out, (0, 2, 1))
-    return (temp_new[:, None], die_power[:, None])
+    )(sc, conduct_table, capacity_table, temp_start, cells_mat, tb, mb, ta, ma, ylo, yhi, cb, ca, dc)
+    return (out[:, None], die_power[:, None])
 
 
 def solution(mesh):

time: 100 us -> 106 us (1.060)
  the two profiles are of different devices: /device:TPU:38 before, /device:TPU:56 now
where the time goes in v3:
time: 106 us; the launch traced here: 105 us
  Pallas kernels  28.8 us (27%)
  starting transfers between devices  27.5 us (26%)
  waiting for transfers between devices  26.5 us (25%)
  local copies, waits for them, and re-layouts  11.6 us (11%)
  other arithmetic  6.77 us (6%)
  between operations  3.53 us (3%)
    pallas_call x1, Pallas kernels, local(): pl.pallas_call(kern, out_shape=jax.ShapeDtypeStruct((local_depth, nx, str...  28.8 us
    ppermute x8, starting transfers between devices, from_behind(): return lax.ppermute(block, axis, route)  23.8 us
    ppermute x3, waiting for transfers between devices, local(): slots.append(lax.ppermute(dl, 'depth', route))  13.4 us
    ppermute x8, waiting for transfers between devices, from_behind(): return lax.ppermute(block, axis, route)  13 us
    unnamed x35, local copies, waits for them, and re-layouts  6.22 us
    ppermute x3, starting transfers between devices, local(): slots.append(lax.ppermute(dl, 'depth', route))  2.22 us
    another operation x1, other arithmetic, local(): dc = jnp.stack(slots)  2.17 us
  transfers between devices with their start and end apart: 14, of which 5 were waited for; matrix products, arithmetic and copies ran while one was open for 11% of the time, Pallas kernels for 0%

profile of v3, /device:TPU:56, one launch (start us, length us, event | category | flops | bytes accessed | tf_op | source)
XLA Modules:
  0.0 104.7 jit_solution(1157148937763837186)
XLA Ops:
  0.7 1.5 %fusion.9 = (s32[1]{0:T(128)}, s32[1]{0:T(128)}, s32[1]{0:T(128)}, s32[1]{0:T(128)}) fusion(s32[4]{0:T(128)} %param.13, s32[]{:T(128)S(6)} %select_n.102, s32[]{:T(128)S(6)} %select_n.107, s32[]{:T(128)S(6)} %select_n.117, s32[]{:T(128)S(6)} %select_n.112), kind=kLoop, calls=%fused_computation.32 | loop fusion | bytes 48 | tf_op jit(solution)/shard_map/dynamic_slice | solution.py:174
  4.7 1.2 %constant_dynamic-slice_fusion.3 = (f32[1,1,256,128]{3,2,1,0:T(8,128)S(1)}, f32[1,1,256,128]{3,2,1,0:T(8,128)S(1)}, f32[1,1,256,128]{3,2,1,0:T(8,128)S(1)}, f32[1,1,256,128]{3,2,1,0:T(8,128)S(1)}) fusion(f32[8,1,256,128]{3,2,1,0:T(8,128)} %param.7, s32[]{:T(128)S(6)} %min.13, s32[]{:T(128)S(6)} %min.15, s32[]{:T(128)S(6)} %min.14, s32[]{:T(128)S(6)} %min.16), kind=kLoop, calls=%fused_computation.30 | loop fusion | bytes 1048592 | tf_op jit(solution)/shard_map/jit(dynamic_index_in_dim)/dynamic_slice | solution.py:175
  8.8 1.0 collective-permute-start.12
  9.7 1.3 %copy.9 = f32[8,1,256,128]{2,3,0,1:T(8,128)} copy(f32[8,1,256,128]{3,2,1,0:T(8,128)S(1)} %copy-done) | data formatting | bytes 2097152 | tf_op args[0]
  11.7 1.1 %copy-done.2 = f32[8,1,256,128]{2,3,0,1:T(8,128)S(1)} copy-done((f32[8,1,256,128]{2,3,0,1:T(8,128)S(1)}, f32[8,1,256,128]{2,3,0,1:T(8,128)}, u32[]{:S(2)}) %copy-start.2) | copy-done | bytes 1048600
  12.9 7.3 %collective-permute-start.5 = (f32[18,6,256]{2,1,0:T(8,128)S(1)}, f32[18,6,256]{2,1,0:T(8,128)S(1)}, u32[]{:S(2)}, u32[]{:S(2)}) collective-permute-start(f32[18,6,256]{2,1,0:T(8,128)S(1)} %get-tuple-element.4), channel_id=1, source_target_pairs={{1,0},{2,1},{3,2},{4,3},{5,4},{6,5},{7,6},{8,7},{9,8},{10,9},{11,1... | collective-permute-start | bytes 331784 | tf_op jit(solution)/shard_map/ppermute | solution.py:24
  20.1 1.9 %collective-permute-start.4 = (f32[18,6,256]{2,1,0:T(8,128)S(1)}, f32[18,6,256]{2,1,0:T(8,128)S(1)}, u32[]{:S(2)}, u32[]{:S(2)}) collective-permute-start(f32[18,6,256]{2,1,0:T(8,128)S(1)} %get-tuple-element.5), channel_id=1, source_target_pairs={{0,1},{1,2},{2,3},{3,4},{4,5},{5,6},{6,7},{7,8},{8,9},{9,10},{10,1... | collective-permute-start | bytes 331784 | tf_op jit(solution)/shard_map/ppermute | solution.py:24
  22.1 1.3 %slice_bitcast_fusion.1 = (f32[6,256,128]{2,1,0:T(8,128)}, f32[6,256,128]{2,1,0:T(8,128)}) fusion(f32[8,1,256,128]{3,2,0,1:T(8,128)S(1)} %bitcast.65), kind=kLoop, calls=%fused_computation.3 | loop fusion | bytes 3145728 | tf_op jit(solution)/shard_map/slice | solution.py:180
  23.8 8.6 %collective-permute-done.4.ylo_ref = f32[18,6,256]{2,1,0:T(8,128)S(1)} collective-permute-done((f32[18,6,256]{2,1,0:T(8,128)S(1)}, f32[18,6,256]{2,1,0:T(8,128)S(1)}, u32[]{:S(2)}, u32[]{:S(2)}) %collective-permute-start.4) | collective-permute-done | bytes 110624 | tf_op jit(solution)/shard_map/ppermute | solution.py:24
  32.5 1.4 %collective-permute-start.10 = (f32[2,144,256]{2,1,0:T(8,128)S(1)}, f32[2,144,256]{2,1,0:T(8,128)S(1)}, u32[]{:S(2)}, u32[]{:S(2)}) collective-permute-start(f32[2,144,256]{2,1,0:T(8,128)S(1)} %concatenate.19), channel_id=1, source_target_pairs={{0,96},{32,0},{64,32},{96,64},{1,97},{33,1},{65,33},{97,65},{2,98}... | collective-permute-start | bytes 884744 | tf_op jit(solution)/shard_map/ppermute | solution.py:207
  35.5 1.9 %collective-permute-start.7 = (f32[2,6,12,256]{3,2,1,0:T(8,128)S(1)}, f32[2,6,12,256]{3,2,1,0:T(8,128)S(1)}, u32[]{:S(2)}, u32[]{:S(2)}) collective-permute-start(f32[2,6,12,256]{3,2,1,0:T(8,128)S(1)} %get-tuple-element.14), channel_id=1, source_target_pairs={{32,0},{64,32},{96,64},{33,1},{65,33},{97,65},{34,2},{66,34},{98,6... | collective-permute-start | bytes 442376 | tf_op jit(solution)/shard_map/ppermute | solution.py:24
  37.4 1.3 %slice_bitcast_fusion = (s32[6,256,128]{2,1,0:T(8,128)}, s32[6,256,128]{2,1,0:T(8,128)}) fusion(s32[8,1,256,128]{3,2,0,1:T(8,128)S(1)} %bitcast.67), kind=kLoop, calls=%fused_computation.2 | loop fusion | bytes 3145728 | tf_op jit(solution)/shard_map/slice | solution.py:181
  38.7 3.2 %collective-permute-start.2 = (f32[6,256,128]{2,1,0:T(8,128)}, f32[6,256,128]{2,1,0:T(8,128)S(1)}, u32[]{:S(2)}, u32[]{:S(2)}) collective-permute-start(f32[6,256,128]{2,1,0:T(8,128)} %get-tuple-element.12), channel_id=1, source_target_pairs={{32,0},{64,32},{96,64},{33,1},{65,33},{97,65},{34,2},{66,34},{98,6... | collective-permute-start | bytes 2359304 | tf_op jit(solution)/shard_map/ppermute | solution.py:24
  42.0 1.9 %collective-permute-start = (f32[6,256,128]{2,1,0:T(8,128)}, f32[6,256,128]{2,1,0:T(8,128)S(1)}, u32[]{:S(2)}, u32[]{:S(2)}) collective-permute-start(f32[6,256,128]{2,1,0:T(8,128)} %get-tuple-element.13), channel_id=1, source_target_pairs={{0,32},{32,64},{64,96},{1,33},{33,65},{65,97},{2,34},{34,66},{66,9... | collective-permute-start | bytes 2359304 | tf_op jit(solution)/shard_map/ppermute | solution.py:24
  43.9 2.6 %collective-permute-done.7.ca_ref = f32[2,6,12,256]{3,2,1,0:T(8,128)S(1)} collective-permute-done((f32[2,6,12,256]{3,2,1,0:T(8,128)S(1)}, f32[2,6,12,256]{3,2,1,0:T(8,128)S(1)}, u32[]{:S(2)}, u32[]{:S(2)}) %collective-permute-start.7) | collective-permute-done | bytes 147488 | tf_op jit(solution)/shard_map/ppermute | solution.py:24
  46.5 3.8 %collective-permute-start.3 = (s32[6,256,128]{2,1,0:T(8,128)}, s32[6,256,128]{2,1,0:T(8,128)S(1)}, u32[]{:S(2)}, u32[]{:S(2)}) collective-permute-start(s32[6,256,128]{2,1,0:T(8,128)} %get-tuple-element.10), channel_id=1, source_target_pairs={{32,0},{64,32},{96,64},{33,1},{65,33},{97,65},{34,2},{66,34},{98,6... | collective-permute-start | bytes 2359304 | tf_op jit(solution)/shard_map/ppermute | solution.py:24
  50.3 1.9 %collective-permute-start.1 = (s32[6,256,128]{2,1,0:T(8,128)}, s32[6,256,128]{2,1,0:T(8,128)}, u32[]{:S(2)}, u32[]{:S(2)}) collective-permute-start(s32[6,256,128]{2,1,0:T(8,128)} %get-tuple-element.11), channel_id=1, source_target_pairs={{0,32},{32,64},{64,96},{1,33},{33,65},{65,97},{2,34},{34,66},{66,9... | collective-permute-start | bytes 2359304 | tf_op jit(solution)/shard_map/ppermute | solution.py:24
  53.8 13.4 %collective-permute-done.8 = f32[2,144,256]{2,1,0:T(8,128)} collective-permute-done((f32[2,144,256]{2,1,0:T(8,128)S(1)}, f32[2,144,256]{2,1,0:T(8,128)}, u32[]{:S(2)}, u32[]{:S(2)}) %collective-permute-start.8) | collective-permute-done | bytes 294944 | tf_op jit(solution)/shard_map/ppermute | solution.py:207
  67.2 1.9 %collective-permute-start.6 = (f32[2,6,12,256]{3,2,1,0:T(8,128)}, f32[2,6,12,256]{3,2,1,0:T(8,128)}, u32[]{:S(2)}, u32[]{:S(2)}) collective-permute-start(f32[2,6,12,256]{3,2,1,0:T(8,128)} %get-tuple-element.15), channel_id=1, source_target_pairs={{0,32},{32,64},{64,96},{1,33},{33,65},{65,97},{2,34},{34,66},{66,9... | collective-permute-start | bytes 442376 | tf_op jit(solution)/shard_map/ppermute | solution.py:24
  69.1 1.1 %fusion.8 = f32[1,1,256,128]{2,3,1,0:T(8,128)S(1)} fusion(f32[1,256,128]{1,2,0:T(8,128)} %collective-permute-done.13, f32[1,256,128]{1,2,0:T(8,128)} %collective-permute-done.12, f32[1,256,128]{1,2,0:T(8,128)} %collective-permute-done.11, f32[1,1,256,128]{2,3,1,0:T(8,128)S(1)} %copy.27, pred[]{:T(512)S(6)} %and.27, f32[1,1,256,128]{2,3,1,0:T(8,128)S(1)} %copy.16, ...), kind=kLoop, calls=%fused_computation.23 | loop fusion | flops 229376 | bytes 917505 | tf_op jit(solution)/shard_map/broadcast_in_dim | solution.py:225
  70.9 2.2 %pad_maximum_fusion.dc_ref = f32[4,2,144,256]{3,2,1,0:T(8,128)} fusion(f32[1,2,144,256]{3,2,1,0:T(8,128)S(1)} %bitcast.77, f32[1,2,144,256]{3,2,1,0:T(8,128)} %bitcast.78, f32[1,2,144,256]{3,2,1,0:T(8,128)} %bitcast.20, f32[1,2,144,256]{3,2,1,0:T(8,128)S(1)} %bitcast.73), kind=kLoop, calls=%fused_computation | loop fusion | flops 884736 | bytes 2359296 | tf_op jit(solution)/shard_map/stack | solution.py:208
  73.1 1.4 %collective-permute-done.6.cb_ref = f32[2,6,12,256]{3,2,1,0:T(8,128)} collective-permute-done((f32[2,6,12,256]{3,2,1,0:T(8,128)}, f32[2,6,12,256]{3,2,1,0:T(8,128)}, u32[]{:S(2)}, u32[]{:S(2)}) %collective-permute-start.6) | collective-permute-done | bytes 147488 | tf_op jit(solution)/shard_map/ppermute | solution.py:24
  74.5 0.9 copy-done.3
  75.9 28.8 %shard_map.86 = f32[8,256,128]{2,1,0:T(8,128)} custom-call(s32[6]{0:T(128)} %pad_add_fusion.sc_ref, f32[8]{0:T(128)} %ctab_ref.1, f32[8]{0:T(128)} %htab_ref.1, f32[8,256,128]{2,1,0:T(8,128)} %bitcast.64, s32[8,256,128]{2,1,0:T(8,128)} %bitcast.66, f32[6,256,128]{2,1,0:T(8,128)} %copy-done.4, s32[6,256,128]{2,1,0:T(8,128)} %collective-permute-done.1.mb_ref, ...), custom_call_target="tpu_custom_call" | custom-call | tf_op jit(solution)/shard_map/pallas_call | solution.py:216
  (60 shorter events, 8.3 us)
Async XLA Ops:
  4.7 5.1 %copy-start = (f32[8,1,256,128]{3,2,1,0:T(8,128)S(1)}, f32[8,1,256,128]{3,2,1,0:T(8,128)}, u32[]{:S(2)}) copy-start(f32[8,1,256,128]{3,2,1,0:T(8,128)} %param.7) | copy-start | bytes 3145732
  6.7 28.8 %collective-permute-start.13 = (f32[1,256,128]{1,2,0:T(8,128)}, f32[1,256,128]{1,2,0:T(8,128)}, u32[]{:S(2)}, u32[]{:S(2)}) collective-permute-start(f32[1,256,128]{1,2,0:T(8,128)} %select_bitcast_fusion), channel_id=1, source_target_pairs={{0,96},{32,0},{64,32},{96,64},{1,97},{33,1},{65,33},{97,65},{2,98}... | collective-permute-start | bytes 393224 | tf_op jit(solution)/shard_map/ppermute | solution.py:185
  7.5 31.3 %collective-permute-start.11 = (f32[1,256,128]{1,2,0:T(8,128)}, f32[1,256,128]{1,2,0:T(8,128)}, u32[]{:S(2)}, u32[]{:S(2)}) collective-permute-start(f32[1,256,128]{1,2,0:T(8,128)} %select_bitcast_fusion.2), channel_id=1, source_target_pairs={{0,32},{32,64},{64,96},{96,0},{1,33},{33,65},{65,97},{97,1},{2,34}... | collective-permute-start | bytes 393224 | tf_op jit(solution)/shard_map/ppermute | solution.py:185
  8.1 3.0 %copy-start.10 = (f32[1,1,256,128]{3,2,1,0:T(8,128)S(1)}, f32[1,1,256,128]{3,2,1,0:T(8,128)}, u32[]{:S(2)}) copy-start(f32[1,1,256,128]{3,2,1,0:T(8,128)} %param.11) | copy-start | bytes 393220
  8.8 2.4 %copy-start.11 = (f32[1,1,256,128]{3,2,1,0:T(8,128)S(1)}, f32[1,1,256,128]{3,2,1,0:T(8,128)}, u32[]{:S(2)}) copy-start(f32[1,1,256,128]{3,2,1,0:T(8,128)} %param.12) | copy-start | bytes 393220
  8.8 2.5 %copy-start.1 = (s32[8,1,256,128]{3,2,1,0:T(8,128)S(1)}, s32[8,1,256,128]{3,2,1,0:T(8,128)}, u32[]{:S(2)}) copy-start(s32[8,1,256,128]{3,2,1,0:T(8,128)} %param.8) | copy-start | bytes 3145732
  8.8 33.2 %collective-permute-start.12 = (f32[1,256,128]{1,2,0:T(8,128)}, f32[1,256,128]{1,2,0:T(8,128)}, u32[]{:S(2)}, u32[]{:S(2)}) collective-permute-start(f32[1,256,128]{1,2,0:T(8,128)} %select_bitcast_fusion.1), channel_id=1, source_target_pairs={{0,64},{32,96},{64,0},{96,32},{1,65},{33,97},{65,1},{97,33},{2,66}... | collective-permute-start | bytes 393224 | tf_op jit(solution)/shard_map/ppermute | solution.py:185
  11.6 1.2 %copy-start.2 = (f32[8,1,256,128]{2,3,0,1:T(8,128)S(1)}, f32[8,1,256,128]{2,3,0,1:T(8,128)}, u32[]{:S(2)}) copy-start(f32[8,1,256,128]{2,3,0,1:T(8,128)} %copy.9) | copy-start | bytes 3145732
  12.9 10.9 %collective-permute-start.5 = (f32[18,6,256]{2,1,0:T(8,128)S(1)}, f32[18,6,256]{2,1,0:T(8,128)S(1)}, u32[]{:S(2)}, u32[]{:S(2)}) collective-permute-start(f32[18,6,256]{2,1,0:T(8,128)S(1)} %get-tuple-element.4), channel_id=1, source_target_pairs={{1,0},{2,1},{3,2},{4,3},{5,4},{6,5},{7,6},{8,7},{9,8},{10,9},{11,1... | collective-permute-start | bytes 331784 | tf_op jit(solution)/shard_map/ppermute | solution.py:24
  20.1 12.3 %collective-permute-start.4 = (f32[18,6,256]{2,1,0:T(8,128)S(1)}, f32[18,6,256]{2,1,0:T(8,128)S(1)}, u32[]{:S(2)}, u32[]{:S(2)}) collective-permute-start(f32[18,6,256]{2,1,0:T(8,128)S(1)} %get-tuple-element.5), channel_id=1, source_target_pairs={{0,1},{1,2},{2,3},{3,4},{4,5},{5,6},{6,7},{7,8},{8,9},{9,10},{10,1... | collective-permute-start | bytes 331784 | tf_op jit(solution)/shard_map/ppermute | solution.py:24
  23.8 15.0 %copy-start.6 = (f32[18,6,256]{2,1,0:T(8,128)}, f32[18,6,256]{2,1,0:T(8,128)S(1)}, u32[]{:S(2)}) copy-start(f32[18,6,256]{2,1,0:T(8,128)S(1)} %collective-permute-done.5.yhi_ref) | copy-start | bytes 331780
  32.4 6.3 %copy-start.7 = (f32[18,6,256]{2,1,0:T(8,128)}, f32[18,6,256]{2,1,0:T(8,128)S(1)}, u32[]{:S(2)}) copy-start(f32[18,6,256]{2,1,0:T(8,128)S(1)} %collective-permute-done.4.ylo_ref) | copy-start | bytes 331780
  32.5 17.9 %collective-permute-start.10 = (f32[2,144,256]{2,1,0:T(8,128)S(1)}, f32[2,144,256]{2,1,0:T(8,128)S(1)}, u32[]{:S(2)}, u32[]{:S(2)}) collective-permute-start(f32[2,144,256]{2,1,0:T(8,128)S(1)} %concatenate.19), channel_id=1, source_target_pairs={{0,96},{32,0},{64,32},{96,64},{1,97},{33,1},{65,33},{97,65},{2,98}... | collective-permute-start | bytes 884744 | tf_op jit(solution)/shard_map/ppermute | solution.py:207
  33.8 18.4 %collective-permute-start.9 = (f32[2,144,256]{2,1,0:T(8,128)S(1)}, f32[2,144,256]{2,1,0:T(8,128)S(1)}, u32[]{:S(2)}, u32[]{:S(2)}) collective-permute-start(f32[2,144,256]{2,1,0:T(8,128)S(1)} %concatenate.19), channel_id=1, source_target_pairs={{0,64},{32,96},{64,0},{96,32},{1,65},{33,97},{65,1},{97,33},{2,66}... | collective-permute-start | bytes 884744 | tf_op jit(solution)/shard_map/ppermute | solution.py:207
  35.5 11.0 %collective-permute-start.7 = (f32[2,6,12,256]{3,2,1,0:T(8,128)S(1)}, f32[2,6,12,256]{3,2,1,0:T(8,128)S(1)}, u32[]{:S(2)}, u32[]{:S(2)}) collective-permute-start(f32[2,6,12,256]{3,2,1,0:T(8,128)S(1)} %get-tuple-element.14), channel_id=1, source_target_pairs={{32,0},{64,32},{96,64},{33,1},{65,33},{97,65},{34,2},{66,34},{98,6... | collective-permute-start | bytes 442376 | tf_op jit(solution)/shard_map/ppermute | solution.py:24
  37.4 15.7 %copy-start.12 = (s32[4]{0:T(128)S(1)}, s32[4]{0:T(128)}, u32[]{:S(2)}) copy-start(s32[4]{0:T(128)} %param.13) | copy-start | bytes 52
  38.7 35.7 %collective-permute-start.2 = (f32[6,256,128]{2,1,0:T(8,128)}, f32[6,256,128]{2,1,0:T(8,128)S(1)}, u32[]{:S(2)}, u32[]{:S(2)}) collective-permute-start(f32[6,256,128]{2,1,0:T(8,128)} %get-tuple-element.12), channel_id=1, source_target_pairs={{32,0},{64,32},{96,64},{33,1},{65,33},{97,65},{34,2},{66,34},{98,6... | collective-permute-start | bytes 2359304 | tf_op jit(solution)/shard_map/ppermute | solution.py:24
  42.0 32.5 %collective-permute-start = (f32[6,256,128]{2,1,0:T(8,128)}, f32[6,256,128]{2,1,0:T(8,128)S(1)}, u32[]{:S(2)}, u32[]{:S(2)}) collective-permute-start(f32[6,256,128]{2,1,0:T(8,128)} %get-tuple-element.13), channel_id=1, source_target_pairs={{0,32},{32,64},{64,96},{1,33},{33,65},{65,97},{2,34},{34,66},{66,9... | collective-permute-start | bytes 2359304 | tf_op jit(solution)/shard_map/ppermute | solution.py:24
  46.5 5.8 %copy-start.9 = (f32[2,6,12,256]{3,2,1,0:T(8,128)}, f32[2,6,12,256]{3,2,1,0:T(8,128)S(1)}, u32[]{:S(2)}) copy-start(f32[2,6,12,256]{3,2,1,0:T(8,128)S(1)} %collective-permute-done.7.ca_ref) | copy-start | bytes 442372
  46.5 28.0 %collective-permute-start.3 = (s32[6,256,128]{2,1,0:T(8,128)}, s32[6,256,128]{2,1,0:T(8,128)S(1)}, u32[]{:S(2)}, u32[]{:S(2)}) collective-permute-start(s32[6,256,128]{2,1,0:T(8,128)} %get-tuple-element.10), channel_id=1, source_target_pairs={{32,0},{64,32},{96,64},{33,1},{65,33},{97,65},{34,2},{66,34},{98,6... | collective-permute-start | bytes 2359304 | tf_op jit(solution)/shard_map/ppermute | solution.py:24
  50.3 24.2 %collective-permute-start.1 = (s32[6,256,128]{2,1,0:T(8,128)}, s32[6,256,128]{2,1,0:T(8,128)}, u32[]{:S(2)}, u32[]{:S(2)}) collective-permute-start(s32[6,256,128]{2,1,0:T(8,128)} %get-tuple-element.11), channel_id=1, source_target_pairs={{0,32},{32,64},{64,96},{1,33},{33,65},{65,97},{2,34},{34,66},{66,9... | collective-permute-start | bytes 2359304 | tf_op jit(solution)/shard_map/ppermute | solution.py:24
  53.0 14.1 %collective-permute-start.8 = (f32[2,144,256]{2,1,0:T(8,128)S(1)}, f32[2,144,256]{2,1,0:T(8,128)}, u32[]{:S(2)}, u32[]{:S(2)}) collective-permute-start(f32[2,144,256]{2,1,0:T(8,128)S(1)} %concatenate.19), channel_id=1, source_target_pairs={{0,32},{32,64},{64,96},{96,0},{1,33},{33,65},{65,97},{97,1},{2,34}... | collective-permute-start | bytes 884744 | tf_op jit(solution)/shard_map/ppermute | solution.py:207
  67.2 7.3 %collective-permute-start.6 = (f32[2,6,12,256]{3,2,1,0:T(8,128)}, f32[2,6,12,256]{3,2,1,0:T(8,128)}, u32[]{:S(2)}, u32[]{:S(2)}) collective-permute-start(f32[2,6,12,256]{3,2,1,0:T(8,128)} %get-tuple-element.15), channel_id=1, source_target_pairs={{0,32},{32,64},{64,96},{1,33},{33,65},{65,97},{2,34},{34,66},{66,9... | collective-permute-start | bytes 442376 | tf_op jit(solution)/shard_map/ppermute | solution.py:24
  74.5 1.4 %copy-start.5 = (s32[6,256,128]{2,1,0:T(8,128)}, s32[6,256,128]{2,1,0:T(8,128)S(1)}, u32[]{:S(2)}) copy-start(s32[6,256,128]{2,1,0:T(8,128)S(1)} %collective-permute-done.3.ma_ref) | copy-start | bytes 2359300
  (3 other events, 2.8 us)
